TPU v7x, 1024 devices: a whole 4x4x32 slice. The times are simulated.
1024 devices in a mesh: dp: 64 (over z, core), expert: 16 (over y, x).
Axes of the slice: x: 4, y: 4, z: 32, core: 2. Of those that a mesh axis runs over, the one named last changes fastest.
Arguments:
- tokens: bfloat16 [131072, 2048], P(('dp', 'expert')), may hold values from -6 to 6
- upstream: bfloat16 [131072, 2048], P(('dp', 'expert')), may hold values from -6 to 6
- expert_ids: int32 [131072, 8], P(('dp', 'expert')), may hold values from 0 to 127, all different within a row; in each aligned block of 128 rows (0 to 127, 128 to 255, ...) at most 10 rows name the same one
- gate_weights: bfloat16 [131072, 8], P(('dp', 'expert')), may hold values from 0.049804688 to 0.5
- w_up: bfloat16 [16, 2048, 768], P('expert'), may hold values from -0.125 to 0.125
- w_down: bfloat16 [16, 768, 2048], P('expert'), may hold values from -0.21875 to 0.21875
Outputs:
- token_grads: bfloat16 [131072, 2048], P(('dp', 'expert'))
- gate_grads: bfloat16 [131072, 8], P(('dp', 'expert'))
- router_grads: float32 [16, 2048], P('expert')
Inputs may be any that keep to these rules, and one draw needn't show every extreme that they name: `expert_ids`: each row names 8 different experts; among the 128 rows of one device no expert is named by more than 10 rows.
All inputs are finite; a program needn't handle non-finite values.
Results may differ from a plain program's by a relative error of at most 0.0063.
Values may be sent and summed in bfloat16 or wider, within the bound.
No kernel may reach another device: no remote copies, remote signals or barrier semaphores. Data moves between devices by JAX's collectives and lax.ppermute only.
A program may use at most 32 MiB of HBM per device.

v0:
```python
import jax
import jax.numpy as jnp
from jax import lax
from jax.sharding import PartitionSpec as P

EXP_DEV = 8


def forward_part(rows_x, up_mat, down_mat):
    act = jnp.dot(rows_x, up_mat, preferred_element_type=jnp.float32)
    sig = jax.nn.sigmoid(act)
    hidden = (act * sig).astype(jnp.bfloat16)
    expert_out = jnp.dot(hidden, down_mat, preferred_element_type=jnp.float32)
    return (act, sig, expert_out)


def scale_part(expert_out, rows_dy, rows_gate):
    dy_wide = rows_dy.astype(jnp.float32)
    gate_term = jnp.sum(dy_wide * expert_out, axis=1)
    scaled = (rows_gate.astype(jnp.float32)[:, None] * dy_wide).astype(jnp.bfloat16)
    return (gate_term, scaled)


def input_part(act, sig, scaled, up_mat, down_mat):
    back = lax.dot_general(
        scaled, down_mat, (((1,), (1,)), ((), ())), preferred_element_type=jnp.float32
    )
    act_grad = (back * sig * (1.0 + act * (1.0 - sig))).astype(jnp.bfloat16)
    return lax.dot_general(
        act_grad, up_mat, (((1,), (1,)), ((), ())), preferred_element_type=jnp.float32
    ).astype(jnp.bfloat16)


def router_total(local_col, column_tok):
    return lax.psum(local_col, "dp") / jnp.float32(column_tok)


def body(tokens, upstream, expert_ids, gate_weights, w_up, w_down):
    owners_count = lax.axis_size("expert")
    experts = EXP_DEV * owners_count
    tok_count = tokens.shape[0]
    top = expert_ids.shape[1]
    width = tokens.shape[1]
    column_tok = tok_count * lax.axis_size("dp")
    most = tok_count * top // experts + tok_count * top // (4 * experts)
    slots_all = owners_count * most
    up_mat = w_up[0]
    down_mat = w_down[0]
    flat_ids = expert_ids.reshape(-1)
    live = flat_ids % EXP_DEV == 0
    target = flat_ids // EXP_DEV
    onehot = ((target[:, None] == jnp.arange(owners_count)[None, :]) & live[:, None]).astype(
        jnp.int32
    )
    before = jnp.cumsum(onehot, axis=0) - onehot
    slot = jnp.sum(before * onehot, axis=1)
    place = jnp.where(live, target * most + slot, -1)
    route_pick = place[None, :] == jnp.arange(slots_all)[:, None]
    token_pick = jnp.any(route_pick.reshape(slots_all, tok_count, top), axis=2).astype(jnp.bfloat16)
    route_table = route_pick.astype(jnp.bfloat16)
    send_x = (
        jnp.dot(token_pick, tokens, preferred_element_type=jnp.float32)
        .astype(jnp.bfloat16)
        .reshape(owners_count, most, width)
    )
    send_dy = (
        jnp.dot(token_pick, upstream, preferred_element_type=jnp.float32)
        .astype(jnp.bfloat16)
        .reshape(owners_count, most, width)
    )
    send_gate = (
        jnp.dot(route_table, gate_weights.reshape(-1), preferred_element_type=jnp.float32)
        .astype(jnp.bfloat16)
        .reshape(owners_count, most)
    )
    rows_x = lax.all_to_all(send_x, "expert", split_axis=0, concat_axis=0, tiled=True)
    rows_dy = lax.all_to_all(send_dy, "expert", split_axis=0, concat_axis=0, tiled=True)
    rows_gate = lax.all_to_all(send_gate, "expert", split_axis=0, concat_axis=0, tiled=True)
    groups = rows_gate.shape[0]
    count = rows_gate.shape[1]
    flat_x = rows_x.reshape(groups * count, width)
    act, sig, expert_out = forward_part(flat_x, up_mat, down_mat)
    gate_term, scaled = scale_part(
        expert_out, rows_dy.reshape(groups * count, width), rows_gate.reshape(-1)
    )
    route_grad = input_part(act, sig, scaled, up_mat, down_mat)
    weighted = (gate_term[:, None] * flat_x.astype(jnp.float32)).reshape(groups, count, width)
    back_rows = lax.all_to_all(
        route_grad.reshape(groups, count, width), "expert", split_axis=0, concat_axis=0, tiled=True
    )
    back_gate = lax.all_to_all(
        gate_term.astype(jnp.bfloat16).reshape(groups, count),
        "expert",
        split_axis=0,
        concat_axis=0,
        tiled=True,
    )
    back_rows, back_gate, weighted_all = (back_rows, back_gate, weighted)
    router_grads = router_total(jnp.sum(weighted_all, axis=(0, 1)), column_tok)
    token_grads = lax.dot_general(
        token_pick,
        back_rows.reshape(slots_all, width),
        (((0,), (0,)), ((), ())),
        preferred_element_type=jnp.float32,
    ).astype(jnp.bfloat16)
    gate_flat = lax.dot_general(
        route_table,
        back_gate.reshape(slots_all),
        (((0,), (0,)), ((), ())),
        preferred_element_type=jnp.float32,
    )
    gate_grads = gate_flat.reshape(tok_count, top).astype(jnp.bfloat16)
    return (token_grads, gate_grads, router_grads[None])


def solution(mesh):
    return jax.shard_map(
        body,
        mesh=mesh,
        in_specs=(
            P(("dp", "expert"), None),
            P(("dp", "expert"), None),
            P(("dp", "expert"), None),
            P(("dp", "expert"), None),
            P("expert", None, None),
            P("expert", None, None),
        ),
        out_specs=(P(("dp", "expert"), None), P(("dp", "expert"), None), P("expert", None)),
        check_vma=False,
    )
```

profile of v0, /device:TPU:2, one launch (start us, length us, event | category | flops | bytes accessed | tf_op | source)
XLA Modules:
  0.0 208.2 jit_solution(5342646416554693753)
XLA Ops:
  0.6 0.0 copy-start
  0.6 0.9 copy.46
  1.6 0.1 reshape.238
  1.7 0.1 reshape.239
  1.8 0.8 copy.55
  2.6 0.1 reshape.250
  2.8 4.5 %reduce-window.6 = s32[16,8,128]{2,1,0:T(8,128)S(1)} reduce-window(s32[16,8,128]{2,1,0:T(8,128)S(1)} %fusion.51, s32[]{:T(128)} %constant.37.clone.1), window={size=1x1x128 pad=0_0x0_0x127_0}, to_apply=%region_0.1 | reduce-window | flops 2080768 | bytes 131076 | tf_op jit(solution)/shard_map/reduce-window
  7.3 0.1 slice.8
  7.4 0.1 copy.52
  7.5 0.1 copy.53
  7.6 0.1 broadcast_add_fusion
  7.7 0.2 fusion.31
  8.0 0.7 all_to_all.25
  8.7 16.4 %all-to-all-start = ((bf16[16,1,10]{2,1,0:T(2,128)(2,1)}), bf16[16,1,10]{2,1,0:T(2,128)(2,1)S(1)}, u32[]{:S(2)}, u32[]{:S(2)}) async-start(bf16[16,1,10]{2,1,0:T(2,128)(2,1)} %all_to_all.25), calls=%async_computation | async-start | bytes 16384 | tf_op jit(solution)/shard_map/all_to_all | solution.py:78
  25.1 0.1 reduce_sum.30
  25.2 0.1 fusion.44
  25.3 0.2 fusion.28
  25.6 2.2 %convolution_convert_fusion.1 = bf16[160,2048]{1,0:T(8,128)(2,1)} fusion(pred[160,128]{1,0:T(8,128)(4,1)S(1)} %fusion.28, bf16[128,2048]{1,0:T(8,128)(2,1)} %param.7), kind=kOutput, calls=%fused_computation.11 | convolution fusion | flops 84213760 | bytes 1200128 | tf_op jit(solution)/shard_map/dot_general | solution.py:67
  27.8 2.2 %reshape.242 = bf16[16,10,2048]{2,1,0:T(8,128)(2,1)} reshape(bf16[160,2048]{1,0:T(8,128)(2,1)} %convolution_convert_fusion.1) | data formatting | bytes 1310720 | tf_op jit(solution)/shard_map/reshape | solution.py:69
  30.0 1.3 all-to-all-done
  31.3 5.9 %all-to-all-start.1 = ((bf16[16,10,2048]{2,1,0:T(8,128)(2,1)}), bf16[16,10,2048]{2,1,0:T(8,128)(2,1)}, u32[]{:S(2)}, u32[]{:S(2)}) async-start(bf16[16,10,2048]{2,1,0:T(8,128)(2,1)} %reshape.242), calls=%async_computation.1 | async-start | bytes 2097152 | tf_op jit(solution)/shard_map/all_to_all | solution.py:77
  37.3 2.2 %convolution_convert_fusion = bf16[160,2048]{1,0:T(8,128)(2,1)} fusion(pred[160,128]{1,0:T(8,128)(4,1)S(1)} %fusion.28, bf16[128,2048]{1,0:T(8,128)(2,1)} %param.6), kind=kOutput, calls=%fused_computation.10 | convolution fusion | flops 84213760 | bytes 1200128 | tf_op jit(solution)/shard_map/dot_general | solution.py:62
  39.5 2.2 %reshape.243 = bf16[16,10,2048]{2,1,0:T(8,128)(2,1)} reshape(bf16[160,2048]{1,0:T(8,128)(2,1)} %convolution_convert_fusion) | data formatting | bytes 1310720 | tf_op jit(solution)/shard_map/reshape | solution.py:64
  41.6 8.3 %all-to-all-done.1 = bf16[16,10,2048]{2,1,0:T(8,128)(2,1)} async-done(((bf16[16,10,2048]{2,1,0:T(8,128)(2,1)}), bf16[16,10,2048]{2,1,0:T(8,128)(2,1)}, u32[]{:S(2)}, u32[]{:S(2)}) %all-to-all-start.1) | async-done | bytes 655392 | tf_op jit(solution)/shard_map/all_to_all | solution.py:77
  50.0 5.7 %all-to-all-start.2 = ((bf16[16,10,2048]{2,1,0:T(8,128)(2,1)}), bf16[16,10,2048]{2,1,0:T(8,128)(2,1)}, u32[]{:S(2)}, u32[]{:S(2)}) async-start(bf16[16,10,2048]{2,1,0:T(8,128)(2,1)} %reshape.243), calls=%async_computation.2 | async-start | bytes 2097152 | tf_op jit(solution)/shard_map/all_to_all | solution.py:76
  55.7 2.5 %multiply_convert_fusion = bf16[16,10,2048]{2,1,0:T(8,128)(2,1)} fusion(f32[16,10]{1,0:T(8,128)S(1)} %bitcast.64, bf16[16,10,2048]{2,1,0:T(8,128)(2,1)} %all-to-all-done.1), kind=kLoop, calls=%fused_computation.14 | loop fusion | flops 983040 | bytes 1311360 | tf_op jit(solution)/shard_map/convert_element_type | solution.py:20
  58.1 2.2 %convert_element_type.84 = bf16[160,2048]{1,0:T(8,128)(2,1)} reshape(bf16[16,10,2048]{2,1,0:T(8,128)(2,1)} %multiply_convert_fusion) | data formatting | bytes 1310720 | tf_op jit(solution)/shard_map/convert_element_type | solution.py:20
  60.3 7.5 %all-to-all-done.2 = bf16[16,10,2048]{2,1,0:T(8,128)(2,1)} async-done(((bf16[16,10,2048]{2,1,0:T(8,128)(2,1)}), bf16[16,10,2048]{2,1,0:T(8,128)(2,1)}, u32[]{:S(2)}, u32[]{:S(2)}) %all-to-all-start.2) | async-done | bytes 655392 | tf_op jit(solution)/shard_map/all_to_all | solution.py:76
  67.8 2.2 %reshape.244 = bf16[160,2048]{1,0:T(8,128)(2,1)} reshape(bf16[16,10,2048]{2,1,0:T(8,128)(2,1)} %all-to-all-done.2) | data formatting | bytes 1310720 | tf_op jit(solution)/shard_map/reshape | solution.py:81
  70.0 0.0 copy-done
  70.0 2.5 %fusion.2 = f32[160,768]{1,0:T(8,128)} fusion(bf16[160,2048]{1,0:T(8,128)(2,1)} %reshape.244, bf16[1,2048,768]{2,1,0:T(8,128)(2,1)S(1)} %copy-done), kind=kOutput, calls=%fused_computation.2 | convolution fusion | flops 503316480 | bytes 4292608 | tf_op jit(solution)/shard_map/dot_general | solution.py:10
  72.5 2.3 %reshape.249 = f32[160,2048]{1,0:T(8,128)} reshape(bf16[16,10,2048]{2,1,0:T(8,128)(2,1)} %all-to-all-done.1) | data formatting | bytes 1966080 | tf_op jit(solution)/shard_map/convert_element_type | solution.py:18
  74.9 3.2 %fusion.14 = f32[160]{0:T(256)S(1)} fusion(f32[160,2048]{1,0:T(8,128)} %reshape.249, bf16[1,768,2048]{2,1,0:T(8,128)(2,1)} %param.11, f32[160,768]{1,0:T(8,128)} %fusion.2), kind=kOutput, calls=%fused_computation.15 | convolution fusion | flops 504586080 | bytes 4948608 | tf_op jit(solution)/shard_map/dot_general | solution.py:13
  78.1 0.7 convert_element_type.98
  78.8 4.8 %all-to-all-start.4 = ((bf16[16,1,10]{2,1,0:T(2,128)(2,1)}), bf16[16,1,10]{2,1,0:T(2,128)(2,1)S(1)}, u32[]{:S(2)}, u32[]{:S(2)}) async-start(bf16[16,1,10]{2,1,0:T(2,128)(2,1)} %convert_element_type.98), calls=%async_computation.4 | async-start | bytes 16384 | tf_op jit(solution)/shard_map/all_to_all | solution.py:91
  83.6 5.4 %fusion.11 = bf16[160,2048]{1,0:T(8,128)(2,1)} fusion(bf16[1,2048,768]{2,1,0:T(8,128)(2,1)S(1)} %copy-done, bf16[160,2048]{1,0:T(8,128)(2,1)} %convert_element_type.84, bf16[1,768,2048]{2,1,0:T(8,128)(2,1)} %param.11, f32[160,768]{1,0:T(8,128)} %fusion.2), kind=kOutput, calls=%fused_computation.9 | convolution fusion | flops 1008066560 | bytes 8093696 | tf_op jit(solution)/shard_map/dot_general | solution.py:29
  89.0 0.1 mul.66
  89.0 2.2 %reshape.245 = bf16[16,10,2048]{2,1,0:T(8,128)(2,1)} reshape(bf16[160,2048]{1,0:T(8,128)(2,1)} %fusion.11) | data formatting | bytes 1310720 | tf_op jit(solution)/shard_map/reshape | solution.py:89
  91.2 0.0 all-to-all-done.4
  91.2 7.3 %all-to-all-start.3 = ((bf16[16,10,2048]{2,1,0:T(8,128)(2,1)}), bf16[16,10,2048]{2,1,0:T(8,128)(2,1)}, u32[]{:S(2)}, u32[]{:S(2)}) async-start(bf16[16,10,2048]{2,1,0:T(8,128)(2,1)} %reshape.245), calls=%async_computation.3 | async-start | bytes 2097152 | tf_op jit(solution)/shard_map/all_to_all | solution.py:88
  98.5 1.5 multiply_reduce_fusion
  100.1 102.3 %psum.7 = f32[2048]{0:T(1024)S(1)} all-reduce(f32[2048]{0:T(1024)S(1)} %multiply_reduce_fusion), channel_id=1, replica_groups=mesh['dp'=64,'expert'=16] {'dp'}, use_global_device_ids=true, to_apply=%region_6.7 | all-reduce | flops 2048 | bytes 16384 | tf_op jit(solution)/shard_map/psum | solution.py:35
  202.4 0.6 broadcast_multiply_fusion
  203.0 0.1 reshape.252
  203.1 0.2 fusion.35
  203.3 0.6 convert_element_type.94
  203.9 0.0 all-to-all-done.3
  203.9 2.1 %reshape.246 = bf16[160,2048]{1,0:T(8,128)(2,1)} reshape(bf16[16,10,2048]{2,1,0:T(8,128)(2,1)} %all-to-all-done.3) | data formatting | bytes 1310720 | tf_op jit(solution)/shard_map/reshape | solution.py:102
  206.0 2.2 %convolution_convert_fusion.2 = bf16[128,2048]{1,0:T(8,128)(2,1)} fusion(pred[160,128]{1,0:T(8,128)(4,1)S(1)} %fusion.28, bf16[160,2048]{1,0:T(8,128)(2,1)} %reshape.246), kind=kOutput, calls=%fused_computation.12 | convolution fusion | flops 84148224 | bytes 1200128 | tf_op jit(solution)/shard_map/dot_general | solution.py:100
  (14 shorter events, 0.2 us)
Async XLA Ops:
  0.6 69.3 %copy-start = (bf16[1,2048,768]{2,1,0:T(8,128)(2,1)S(1)}, bf16[1,2048,768]{2,1,0:T(8,128)(2,1)}, u32[]{:S(2)}) copy-start(bf16[1,2048,768]{2,1,0:T(8,128)(2,1)} %param.10) | copy-start | bytes 9437188
  8.7 22.6 %all-to-all-start = ((bf16[16,1,10]{2,1,0:T(2,128)(2,1)}), bf16[16,1,10]{2,1,0:T(2,128)(2,1)S(1)}, u32[]{:S(2)}, u32[]{:S(2)}) async-start(bf16[16,1,10]{2,1,0:T(2,128)(2,1)} %all_to_all.25), calls=%async_computation | async-start | bytes 16384 | tf_op jit(solution)/shard_map/all_to_all | solution.py:78
  31.3 18.7 %all-to-all-start.1 = ((bf16[16,10,2048]{2,1,0:T(8,128)(2,1)}), bf16[16,10,2048]{2,1,0:T(8,128)(2,1)}, u32[]{:S(2)}, u32[]{:S(2)}) async-start(bf16[16,10,2048]{2,1,0:T(8,128)(2,1)} %reshape.242), calls=%async_computation.1 | async-start | bytes 2097152 | tf_op jit(solution)/shard_map/all_to_all | solution.py:77
  50.0 17.8 %all-to-all-start.2 = ((bf16[16,10,2048]{2,1,0:T(8,128)(2,1)}), bf16[16,10,2048]{2,1,0:T(8,128)(2,1)}, u32[]{:S(2)}, u32[]{:S(2)}) async-start(bf16[16,10,2048]{2,1,0:T(8,128)(2,1)} %reshape.243), calls=%async_computation.2 | async-start | bytes 2097152 | tf_op jit(solution)/shard_map/all_to_all | solution.py:76
  78.8 12.4 %all-to-all-start.4 = ((bf16[16,1,10]{2,1,0:T(2,128)(2,1)}), bf16[16,1,10]{2,1,0:T(2,128)(2,1)S(1)}, u32[]{:S(2)}, u32[]{:S(2)}) async-start(bf16[16,1,10]{2,1,0:T(2,128)(2,1)} %convert_element_type.98), calls=%async_computation.4 | async-start | bytes 16384 | tf_op jit(solution)/shard_map/all_to_all | solution.py:91
  91.2 112.6 %all-to-all-start.3 = ((bf16[16,10,2048]{2,1,0:T(8,128)(2,1)}), bf16[16,10,2048]{2,1,0:T(8,128)(2,1)}, u32[]{:S(2)}, u32[]{:S(2)}) async-start(bf16[16,10,2048]{2,1,0:T(8,128)(2,1)} %reshape.245), calls=%async_computation.3 | async-start | bytes 2097152 | tf_op jit(solution)/shard_map/all_to_all | solution.py:88
where the time goes:
time: 210 us; the launch traced here: 208 us
  blocking collectives  102 us (49%)
  starting transfers between devices  40.1 us (19%)
  local copies, waits for them, and re-layouts  19.4 us (9%)
  matrix products  18.2 us (9%)
  waiting for transfers between devices  17.2 us (8%)
  other arithmetic  10.3 us (5%)
    psum x1, blocking collectives, router_total(): return lax.psum(local_col, 'dp') / jnp.float32(column_tok)  102 us
    all_to_all x1, starting transfers between devices, body(): lax.all_to_all(send_gate, 'expert', split_axis=0, concat_axis=0, tiled=True)  16.4 us
    all_to_all x1, waiting for transfers between devices, body(): lax.all_to_all(send_dy, 'expert', split_axis=0, concat_axis=0, tiled=True)  8.32 us
    all_to_all x1, waiting for transfers between devices, body(): lax.all_to_all(send_x, 'expert', split_axis=0, concat_axis=0, tiled=True)  7.51 us
    all_to_all x1, starting transfers between devices, body(): lax.all_to_all(route_grad.reshape(groups, count, width), 'expert', split_...  7.28 us
    all_to_all x1, starting transfers between devices, body(): lax.all_to_all(send_dy, 'expert', split_axis=0, concat_axis=0, tiled=True)  5.95 us
    all_to_all x1, starting transfers between devices, body(): lax.all_to_all(send_x, 'expert', split_axis=0, concat_axis=0, tiled=True)  5.69 us
    dot_general x1, matrix products, input_part(): lax.dot_general(act_grad, up_mat, (((1,), (1,)), ((), ())), preferred_ele...  5.41 us
  transfers between devices with their start and end apart: 5, of which 3 were waited for; matrix products, arithmetic and copies ran while one was open for 12% of the time, Pallas kernels for 0%

commit v1 on v0

--- a/solution.py
+++ b/solution.py
@@ -32,7 +32,14 @@
 
 
 def router_total(local_col, column_tok):
-    return lax.psum(local_col, "dp") / jnp.float32(column_tok)
+    n = lax.axis_size("dp")
+    acc = local_col
+    d = 1
+    while d < n:
+        perm = [(i, i ^ d) for i in range(n)]
+        acc = acc + lax.ppermute(acc, "dp", perm)
+        d *= 2
+    return acc / jnp.float32(column_tok)
 
 
 def body(tokens, upstream, expert_ids, gate_weights, w_up, w_down):

time: 210 us -> 172 us (0.82)
  blocking collectives: 102 us -> 0 us
  starting transfers between devices: 40.1 us -> 89.2 us
  waiting for transfers between devices: 17.2 us -> 32.6 us
    psum x1 -> x0, blocking collectives: 102 us -> none  [router_total(): return lax.psum(local_col, 'dp') / jnp.float32(column_tok)]
    ppermute x0 -> x6, starting transfers between devices: none -> 49.1 us  [router_total(): acc = acc + lax.ppermute(acc, 'dp', perm)]
    ppermute x0 -> x6, waiting for transfers between devices: none -> 15.4 us  [router_total(): acc = acc + lax.ppermute(acc, 'dp', perm)]
  transfers between devices with their start and end apart: 5 -> 11, of which waited for: 3 -> 9; matrix products, arithmetic and copies ran while one was open for 12% -> 14% of each run, Pallas kernels for 0% -> 0%
where the time goes in v1:
time: 172 us; the launch traced here: 171 us
  starting transfers between devices  89.2 us (52%)
  waiting for transfers between devices  32.6 us (19%)
  local copies, waits for them, and re-layouts  19.4 us (11%)
  matrix products  18.2 us (11%)
  other arithmetic  10.3 us (6%)
    ppermute x6, starting transfers between devices, router_total(): acc = acc + lax.ppermute(acc, 'dp', perm)  49.1 us
    all_to_all x1, starting transfers between devices, body(): lax.all_to_all(send_gate, 'expert', split_axis=0, concat_axis=0, tiled=True)  16.4 us
    ppermute x6, waiting for transfers between devices, router_total(): acc = acc + lax.ppermute(acc, 'dp', perm)  15.4 us
    all_to_all x1, waiting for transfers between devices, body(): lax.all_to_all(send_dy, 'expert', split_axis=0, concat_axis=0, tiled=True)  8.33 us
    all_to_all x1, waiting for transfers between devices, body(): lax.all_to_all(send_x, 'expert', split_axis=0, concat_axis=0, tiled=True)  7.51 us
    all_to_all x1, starting transfers between devices, body(): lax.all_to_all(route_grad.reshape(groups, count, width), 'expert', split_...  7.28 us
    all_to_all x1, starting transfers between devices, body(): lax.all_to_all(send_dy, 'expert', split_axis=0, concat_axis=0, tiled=True)  5.94 us
    all_to_all x1, starting transfers between devices, body(): lax.all_to_all(send_x, 'expert', split_axis=0, concat_axis=0, tiled=True)  5.68 us
  transfers between devices with their start and end apart: 11, of which 9 were waited for; matrix products, arithmetic and copies ran while one was open for 14% of the time, Pallas kernels for 0%

profile of v1, /device:TPU:2, one launch (start us, length us, event | category | flops | bytes accessed | tf_op | source)
XLA Modules:
  0.0 170.5 jit_solution(13927350728015408719)
XLA Ops:
  0.6 0.0 copy-start
  0.6 0.9 copy.46
  1.6 0.1 reshape.239
  1.7 0.1 reshape.238
  1.9 4.5 %reduce-window.6 = s32[16,8,128]{2,1,0:T(8,128)S(1)} reduce-window(s32[16,8,128]{2,1,0:T(8,128)S(1)} %fusion.51, s32[]{:T(128)} %constant.37.clone.1), window={size=1x1x128 pad=0_0x0_0x127_0}, to_apply=%region_0.1 | reduce-window | flops 2080768 | bytes 131076 | tf_op jit(solution)/shard_map/reduce-window
  6.4 0.1 slice.8
  6.4 0.1 copy.52
  6.6 0.1 copy.53
  6.7 0.1 broadcast_add_fusion
  6.8 0.8 copy.55
  7.6 0.1 reshape.250
  7.7 0.2 fusion.31
  8.0 0.7 all_to_all.25
  8.7 16.4 %all-to-all-start = ((bf16[16,1,10]{2,1,0:T(2,128)(2,1)}), bf16[16,1,10]{2,1,0:T(2,128)(2,1)S(1)}, u32[]{:S(2)}, u32[]{:S(2)}) async-start(bf16[16,1,10]{2,1,0:T(2,128)(2,1)} %all_to_all.25), calls=%async_computation | async-start | bytes 16384 | tf_op jit(solution)/shard_map/all_to_all | solution.py:85
  25.1 0.1 reduce_sum.30
  25.2 0.1 fusion.44
  25.3 0.2 fusion.28
  25.6 2.2 %convolution_convert_fusion.1 = bf16[160,2048]{1,0:T(8,128)(2,1)} fusion(pred[160,128]{1,0:T(8,128)(4,1)S(1)} %fusion.28, bf16[128,2048]{1,0:T(8,128)(2,1)} %param.7), kind=kOutput, calls=%fused_computation.11 | convolution fusion | flops 84213760 | bytes 1200128 | tf_op jit(solution)/shard_map/dot_general | solution.py:74
  27.8 2.2 %reshape.242 = bf16[16,10,2048]{2,1,0:T(8,128)(2,1)} reshape(bf16[160,2048]{1,0:T(8,128)(2,1)} %convolution_convert_fusion.1) | data formatting | bytes 1310720 | tf_op jit(solution)/shard_map/reshape | solution.py:76
  30.0 1.3 all-to-all-done
  31.3 5.9 %all-to-all-start.1 = ((bf16[16,10,2048]{2,1,0:T(8,128)(2,1)}), bf16[16,10,2048]{2,1,0:T(8,128)(2,1)}, u32[]{:S(2)}, u32[]{:S(2)}) async-start(bf16[16,10,2048]{2,1,0:T(8,128)(2,1)} %reshape.242), calls=%async_computation.1 | async-start | bytes 2097152 | tf_op jit(solution)/shard_map/all_to_all | solution.py:84
  37.3 2.2 %convolution_convert_fusion = bf16[160,2048]{1,0:T(8,128)(2,1)} fusion(pred[160,128]{1,0:T(8,128)(4,1)S(1)} %fusion.28, bf16[128,2048]{1,0:T(8,128)(2,1)} %param.6), kind=kOutput, calls=%fused_computation.10 | convolution fusion | flops 84213760 | bytes 1200128 | tf_op jit(solution)/shard_map/dot_general | solution.py:69
  39.5 2.2 %reshape.243 = bf16[16,10,2048]{2,1,0:T(8,128)(2,1)} reshape(bf16[160,2048]{1,0:T(8,128)(2,1)} %convolution_convert_fusion) | data formatting | bytes 1310720 | tf_op jit(solution)/shard_map/reshape | solution.py:71
  41.6 8.3 %all-to-all-done.1 = bf16[16,10,2048]{2,1,0:T(8,128)(2,1)} async-done(((bf16[16,10,2048]{2,1,0:T(8,128)(2,1)}), bf16[16,10,2048]{2,1,0:T(8,128)(2,1)}, u32[]{:S(2)}, u32[]{:S(2)}) %all-to-all-start.1) | async-done | bytes 655392 | tf_op jit(solution)/shard_map/all_to_all | solution.py:84
  50.0 5.7 %all-to-all-start.2 = ((bf16[16,10,2048]{2,1,0:T(8,128)(2,1)}), bf16[16,10,2048]{2,1,0:T(8,128)(2,1)}, u32[]{:S(2)}, u32[]{:S(2)}) async-start(bf16[16,10,2048]{2,1,0:T(8,128)(2,1)} %reshape.243), calls=%async_computation.2 | async-start | bytes 2097152 | tf_op jit(solution)/shard_map/all_to_all | solution.py:83
  55.7 2.5 %multiply_convert_fusion = bf16[16,10,2048]{2,1,0:T(8,128)(2,1)} fusion(f32[16,10]{1,0:T(8,128)S(1)} %bitcast.64, bf16[16,10,2048]{2,1,0:T(8,128)(2,1)} %all-to-all-done.1), kind=kLoop, calls=%fused_computation.14 | loop fusion | flops 983040 | bytes 1311360 | tf_op jit(solution)/shard_map/convert_element_type | solution.py:20
  58.1 2.2 %convert_element_type.84 = bf16[160,2048]{1,0:T(8,128)(2,1)} reshape(bf16[16,10,2048]{2,1,0:T(8,128)(2,1)} %multiply_convert_fusion) | data formatting | bytes 1310720 | tf_op jit(solution)/shard_map/convert_element_type | solution.py:20
  60.3 7.5 %all-to-all-done.2 = bf16[16,10,2048]{2,1,0:T(8,128)(2,1)} async-done(((bf16[16,10,2048]{2,1,0:T(8,128)(2,1)}), bf16[16,10,2048]{2,1,0:T(8,128)(2,1)}, u32[]{:S(2)}, u32[]{:S(2)}) %all-to-all-start.2) | async-done | bytes 655392 | tf_op jit(solution)/shard_map/all_to_all | solution.py:83
  67.8 2.2 %reshape.244 = bf16[160,2048]{1,0:T(8,128)(2,1)} reshape(bf16[16,10,2048]{2,1,0:T(8,128)(2,1)} %all-to-all-done.2) | data formatting | bytes 1310720 | tf_op jit(solution)/shard_map/reshape | solution.py:88
  70.0 0.0 copy-done
  70.0 2.5 %fusion.2 = f32[160,768]{1,0:T(8,128)} fusion(bf16[160,2048]{1,0:T(8,128)(2,1)} %reshape.244, bf16[1,2048,768]{2,1,0:T(8,128)(2,1)S(1)} %copy-done), kind=kOutput, calls=%fused_computation.2 | convolution fusion | flops 503316480 | bytes 4292608 | tf_op jit(solution)/shard_map/dot_general | solution.py:10
  72.5 2.3 %reshape.249 = f32[160,2048]{1,0:T(8,128)} reshape(bf16[16,10,2048]{2,1,0:T(8,128)(2,1)} %all-to-all-done.1) | data formatting | bytes 1966080 | tf_op jit(solution)/shard_map/convert_element_type | solution.py:18
  74.9 3.2 %fusion.14 = f32[160]{0:T(256)S(1)} fusion(f32[160,2048]{1,0:T(8,128)} %reshape.249, bf16[1,768,2048]{2,1,0:T(8,128)(2,1)} %param.11, f32[160,768]{1,0:T(8,128)} %fusion.2), kind=kOutput, calls=%fused_computation.15 | convolution fusion | flops 504586080 | bytes 4948608 | tf_op jit(solution)/shard_map/dot_general | solution.py:13
  78.1 0.7 convert_element_type.98
  78.8 4.7 %all-to-all-start.4 = ((bf16[16,1,10]{2,1,0:T(2,128)(2,1)}), bf16[16,1,10]{2,1,0:T(2,128)(2,1)S(1)}, u32[]{:S(2)}, u32[]{:S(2)}) async-start(bf16[16,1,10]{2,1,0:T(2,128)(2,1)} %convert_element_type.98), calls=%async_computation.4 | async-start | bytes 16384 | tf_op jit(solution)/shard_map/all_to_all | solution.py:98
  83.5 5.4 %fusion.11 = bf16[160,2048]{1,0:T(8,128)(2,1)} fusion(bf16[1,2048,768]{2,1,0:T(8,128)(2,1)S(1)} %copy-done, bf16[160,2048]{1,0:T(8,128)(2,1)} %convert_element_type.84, bf16[1,768,2048]{2,1,0:T(8,128)(2,1)} %param.11, f32[160,768]{1,0:T(8,128)} %fusion.2), kind=kOutput, calls=%fused_computation.9 | convolution fusion | flops 1008066560 | bytes 8093696 | tf_op jit(solution)/shard_map/dot_general | solution.py:29
  88.9 0.1 mul.66
  89.0 2.2 %reshape.245 = bf16[16,10,2048]{2,1,0:T(8,128)(2,1)} reshape(bf16[160,2048]{1,0:T(8,128)(2,1)} %fusion.11) | data formatting | bytes 1310720 | tf_op jit(solution)/shard_map/reshape | solution.py:96
  91.2 0.0 all-to-all-done.4
  91.2 7.3 %all-to-all-start.3 = ((bf16[16,10,2048]{2,1,0:T(8,128)(2,1)}), bf16[16,10,2048]{2,1,0:T(8,128)(2,1)}, u32[]{:S(2)}, u32[]{:S(2)}) async-start(bf16[16,10,2048]{2,1,0:T(8,128)(2,1)} %reshape.245), calls=%async_computation.3 | async-start | bytes 2097152 | tf_op jit(solution)/shard_map/all_to_all | solution.py:95
  98.5 1.5 multiply_reduce_fusion
  100.1 1.9 %collective-permute-start = (f32[2048]{0:T(1024)S(1)}, f32[2048]{0:T(1024)S(1)}, u32[]{:S(2)}, u32[]{:S(2)}) collective-permute-start(f32[2048]{0:T(1024)S(1)} %multiply_reduce_fusion), channel_id=1, source_target_pairs={{0,16},{16,0},{32,48},{48,32},{64,80},{80,64},{96,112},{112,96},{1... | collective-permute-start | bytes 24584 | tf_op jit(solution)/shard_map/ppermute | solution.py:40
  102.0 1.1 collective-permute-done
  103.1 1.9 %collective-permute-start.1 = (f32[2048]{0:T(1024)S(1)}, f32[2048]{0:T(1024)S(1)}, u32[]{:S(2)}, u32[]{:S(2)}) collective-permute-start(f32[2048]{0:T(1024)S(1)} %add.75), channel_id=1, source_target_pairs={{0,32},{16,48},{32,0},{48,16},{64,96},{80,112},{96,64},{112,80},{1... | collective-permute-start | bytes 24584 | tf_op jit(solution)/shard_map/ppermute | solution.py:40
  105.0 3.6 %collective-permute-done.1 = f32[2048]{0:T(1024)S(1)} collective-permute-done((f32[2048]{0:T(1024)S(1)}, f32[2048]{0:T(1024)S(1)}, u32[]{:S(2)}, u32[]{:S(2)}) %collective-permute-start.1) | collective-permute-done | bytes 8224 | tf_op jit(solution)/shard_map/ppermute | solution.py:40
  108.7 1.9 %collective-permute-start.2 = (f32[2048]{0:T(1024)S(1)}, f32[2048]{0:T(1024)S(1)}, u32[]{:S(2)}, u32[]{:S(2)}) collective-permute-start(f32[2048]{0:T(1024)S(1)} %add.76), channel_id=1, source_target_pairs={{0,64},{16,80},{32,96},{48,112},{64,0},{80,16},{96,32},{112,48},{1... | collective-permute-start | bytes 24584 | tf_op jit(solution)/shard_map/ppermute | solution.py:40
  110.6 4.5 %collective-permute-done.2 = f32[2048]{0:T(1024)S(1)} collective-permute-done((f32[2048]{0:T(1024)S(1)}, f32[2048]{0:T(1024)S(1)}, u32[]{:S(2)}, u32[]{:S(2)}) %collective-permute-start.2) | collective-permute-done | bytes 8224 | tf_op jit(solution)/shard_map/ppermute | solution.py:40
  115.1 5.6 %collective-permute-start.3 = (f32[2048]{0:T(1024)S(1)}, f32[2048]{0:T(1024)S(1)}, u32[]{:S(2)}, u32[]{:S(2)}) collective-permute-start(f32[2048]{0:T(1024)S(1)} %add.77), channel_id=1, source_target_pairs={{0,128},{16,144},{32,160},{48,176},{64,192},{80,208},{96,224},{112... | collective-permute-start | bytes 24584 | tf_op jit(solution)/shard_map/ppermute | solution.py:40
  120.8 3.8 %collective-permute-done.3 = f32[2048]{0:T(1024)S(1)} collective-permute-done((f32[2048]{0:T(1024)S(1)}, f32[2048]{0:T(1024)S(1)}, u32[]{:S(2)}, u32[]{:S(2)}) %collective-permute-start.3) | collective-permute-done | bytes 8224 | tf_op jit(solution)/shard_map/ppermute | solution.py:40
  124.5 13.5 %collective-permute-start.4 = (f32[2048]{0:T(1024)S(1)}, f32[2048]{0:T(1024)S(1)}, u32[]{:S(2)}, u32[]{:S(2)}) collective-permute-start(f32[2048]{0:T(1024)S(1)} %add.78), channel_id=1, source_target_pairs={{0,256},{16,272},{32,288},{48,304},{64,320},{80,336},{96,352},{112... | collective-permute-start | bytes 24584 | tf_op jit(solution)/shard_map/ppermute | solution.py:40
  138.1 0.1 reshape.252
  138.2 1.5 collective-permute-done.4
  139.7 24.3 %collective-permute-start.5 = (f32[2048]{0:T(1024)S(1)}, f32[2048]{0:T(1024)S(1)}, u32[]{:S(2)}, u32[]{:S(2)}) collective-permute-start(f32[2048]{0:T(1024)S(1)} %add.79), channel_id=1, source_target_pairs={{0,512},{16,528},{32,544},{48,560},{64,576},{80,592},{96,608},{112... | collective-permute-start | bytes 24584 | tf_op jit(solution)/shard_map/ppermute | solution.py:40
  163.9 0.2 fusion.35
  164.1 0.6 convert_element_type.94
  164.7 0.9 collective-permute-done.5
  165.5 0.6 add_multiply_fusion
  166.2 0.0 all-to-all-done.3
  166.2 2.1 %reshape.246 = bf16[160,2048]{1,0:T(8,128)(2,1)} reshape(bf16[16,10,2048]{2,1,0:T(8,128)(2,1)} %all-to-all-done.3) | data formatting | bytes 1310720 | tf_op jit(solution)/shard_map/reshape | solution.py:109
  168.3 2.2 %convolution_convert_fusion.2 = bf16[128,2048]{1,0:T(8,128)(2,1)} fusion(pred[160,128]{1,0:T(8,128)(4,1)S(1)} %fusion.28, bf16[160,2048]{1,0:T(8,128)(2,1)} %reshape.246), kind=kOutput, calls=%fused_computation.12 | convolution fusion | flops 84148224 | bytes 1200128 | tf_op jit(solution)/shard_map/dot_general | solution.py:107
  (19 shorter events, 0.3 us)
Async XLA Ops:
  0.6 69.3 %copy-start = (bf16[1,2048,768]{2,1,0:T(8,128)(2,1)S(1)}, bf16[1,2048,768]{2,1,0:T(8,128)(2,1)}, u32[]{:S(2)}) copy-start(bf16[1,2048,768]{2,1,0:T(8,128)(2,1)} %param.10) | copy-start | bytes 9437188
  8.7 22.6 %all-to-all-start = ((bf16[16,1,10]{2,1,0:T(2,128)(2,1)}), bf16[16,1,10]{2,1,0:T(2,128)(2,1)S(1)}, u32[]{:S(2)}, u32[]{:S(2)}) async-start(bf16[16,1,10]{2,1,0:T(2,128)(2,1)} %all_to_all.25), calls=%async_computation | async-start | bytes 16384 | tf_op jit(solution)/shard_map/all_to_all | solution.py:85
  31.3 18.7 %all-to-all-start.1 = ((bf16[16,10,2048]{2,1,0:T(8,128)(2,1)}), bf16[16,10,2048]{2,1,0:T(8,128)(2,1)}, u32[]{:S(2)}, u32[]{:S(2)}) async-start(bf16[16,10,2048]{2,1,0:T(8,128)(2,1)} %reshape.242), calls=%async_computation.1 | async-start | bytes 2097152 | tf_op jit(solution)/shard_map/all_to_all | solution.py:84
  50.0 17.8 %all-to-all-start.2 = ((bf16[16,10,2048]{2,1,0:T(8,128)(2,1)}), bf16[16,10,2048]{2,1,0:T(8,128)(2,1)}, u32[]{:S(2)}, u32[]{:S(2)}) async-start(bf16[16,10,2048]{2,1,0:T(8,128)(2,1)} %reshape.243), calls=%async_computation.2 | async-start | bytes 2097152 | tf_op jit(solution)/shard_map/all_to_all | solution.py:83
  78.8 12.4 %all-to-all-start.4 = ((bf16[16,1,10]{2,1,0:T(2,128)(2,1)}), bf16[16,1,10]{2,1,0:T(2,128)(2,1)S(1)}, u32[]{:S(2)}, u32[]{:S(2)}) async-start(bf16[16,1,10]{2,1,0:T(2,128)(2,1)} %convert_element_type.98), calls=%async_computation.4 | async-start | bytes 16384 | tf_op jit(solution)/shard_map/all_to_all | solution.py:98
  91.2 74.9 %all-to-all-start.3 = ((bf16[16,10,2048]{2,1,0:T(8,128)(2,1)}), bf16[16,10,2048]{2,1,0:T(8,128)(2,1)}, u32[]{:S(2)}, u32[]{:S(2)}) async-start(bf16[16,10,2048]{2,1,0:T(8,128)(2,1)} %reshape.245), calls=%async_computation.3 | async-start | bytes 2097152 | tf_op jit(solution)/shard_map/all_to_all | solution.py:95
  100.1 3.1 %collective-permute-start = (f32[2048]{0:T(1024)S(1)}, f32[2048]{0:T(1024)S(1)}, u32[]{:S(2)}, u32[]{:S(2)}) collective-permute-start(f32[2048]{0:T(1024)S(1)} %multiply_reduce_fusion), channel_id=1, source_target_pairs={{0,16},{16,0},{32,48},{48,32},{64,80},{80,64},{96,112},{112,96},{1... | collective-permute-start | bytes 24584 | tf_op jit(solution)/shard_map/ppermute | solution.py:40
  103.1 5.5 %collective-permute-start.1 = (f32[2048]{0:T(1024)S(1)}, f32[2048]{0:T(1024)S(1)}, u32[]{:S(2)}, u32[]{:S(2)}) collective-permute-start(f32[2048]{0:T(1024)S(1)} %add.75), channel_id=1, source_target_pairs={{0,32},{16,48},{32,0},{48,16},{64,96},{80,112},{96,64},{112,80},{1... | collective-permute-start | bytes 24584 | tf_op jit(solution)/shard_map/ppermute | solution.py:40
  108.7 6.4 %collective-permute-start.2 = (f32[2048]{0:T(1024)S(1)}, f32[2048]{0:T(1024)S(1)}, u32[]{:S(2)}, u32[]{:S(2)}) collective-permute-start(f32[2048]{0:T(1024)S(1)} %add.76), channel_id=1, source_target_pairs={{0,64},{16,80},{32,96},{48,112},{64,0},{80,16},{96,32},{112,48},{1... | collective-permute-start | bytes 24584 | tf_op jit(solution)/shard_map/ppermute | solution.py:40
  115.1 9.4 %collective-permute-start.3 = (f32[2048]{0:T(1024)S(1)}, f32[2048]{0:T(1024)S(1)}, u32[]{:S(2)}, u32[]{:S(2)}) collective-permute-start(f32[2048]{0:T(1024)S(1)} %add.77), channel_id=1, source_target_pairs={{0,128},{16,144},{32,160},{48,176},{64,192},{80,208},{96,224},{112... | collective-permute-start | bytes 24584 | tf_op jit(solution)/shard_map/ppermute | solution.py:40
  124.5 15.1 %collective-permute-start.4 = (f32[2048]{0:T(1024)S(1)}, f32[2048]{0:T(1024)S(1)}, u32[]{:S(2)}, u32[]{:S(2)}) collective-permute-start(f32[2048]{0:T(1024)S(1)} %add.78), channel_id=1, source_target_pairs={{0,256},{16,272},{32,288},{48,304},{64,320},{80,336},{96,352},{112... | collective-permute-start | bytes 24584 | tf_op jit(solution)/shard_map/ppermute | solution.py:40
  139.7 25.9 %collective-permute-start.5 = (f32[2048]{0:T(1024)S(1)}, f32[2048]{0:T(1024)S(1)}, u32[]{:S(2)}, u32[]{:S(2)}) collective-permute-start(f32[2048]{0:T(1024)S(1)} %add.79), channel_id=1, source_target_pairs={{0,512},{16,528},{32,544},{48,560},{64,576},{80,592},{96,608},{112... | collective-permute-start | bytes 24584 | tf_op jit(solution)/shard_map/ppermute | solution.py:40

commit v2 on v1

v2 whole, which is shorter than its diff:
```python
import jax
import jax.numpy as jnp
from jax import lax
from jax.sharding import PartitionSpec as P

EXP_DEV = 8
DP_REDUCE = "a2a"


def dp_sum(local_col):
    n = lax.axis_size("dp")
    width = local_col.shape[0]
    if DP_REDUCE == "a2a":
        parts = local_col.reshape(n, width // n)
        mine = jnp.sum(lax.all_to_all(parts, "dp", 0, 0, tiled=True), axis=0)
        spread = jnp.broadcast_to(mine[None], (n, width // n))
        return lax.all_to_all(spread, "dp", 0, 0, tiled=True).reshape(width)
    acc = local_col
    d = 1
    while d < n:
        acc = acc + lax.ppermute(acc, "dp", [(i, i ^ d) for i in range(n)])
        d *= 2
    return acc


def body(tokens, upstream, expert_ids, gate_weights, w_up, w_down):
    owners = lax.axis_size("expert")
    experts = EXP_DEV * owners
    tok_count, top = expert_ids.shape
    width = tokens.shape[1]
    column_tok = tok_count * lax.axis_size("dp")
    most = tok_count * top // experts + tok_count * top // (4 * experts)
    up_mat = w_up[0]
    down_mat = w_down[0]
    live = expert_ids % EXP_DEV == 0
    target = expert_ids // EXP_DEV
    hit = (target[:, :, None] == jnp.arange(owners)[None, None, :]) & live[:, :, None]
    hit_f = hit.astype(jnp.float32)
    tok_oh = jnp.sum(hit_f, axis=1)
    lower = (jnp.arange(tok_count)[None, :] < jnp.arange(tok_count)[:, None]).astype(jnp.float32)
    before = jnp.dot(lower, tok_oh, preferred_element_type=jnp.float32)
    slot_hit = before.T[:, None, :] == jnp.arange(most, dtype=jnp.float32)[None, :, None]
    pick = (slot_hit & (tok_oh.T[:, None, :] > 0)).astype(jnp.bfloat16)
    gate_tc = jnp.sum(hit_f * gate_weights.astype(jnp.float32)[:, :, None], axis=1)
    send_x = jnp.einsum("cst,td->csd", pick, tokens, preferred_element_type=jnp.float32)
    send_dy = jnp.einsum("cst,td->csd", pick, upstream, preferred_element_type=jnp.float32)
    send_gate = jnp.einsum(
        "cst,tc->cs", pick.astype(jnp.float32), gate_tc, preferred_element_type=jnp.float32
    )
    gate_cols = jnp.broadcast_to(send_gate[:, :, None], (owners, most, 128))
    packed = jnp.concatenate([send_x, send_dy, gate_cols], axis=2).astype(jnp.bfloat16)
    recv = lax.all_to_all(packed, "expert", 0, 0, tiled=True)
    rows_x = recv[:, :, :width]
    rows_dy = recv[:, :, width : 2 * width]
    rows_gate = recv[:, :, 2 * width]
    act = jnp.einsum("gsd,df->gsf", rows_x, up_mat, preferred_element_type=jnp.float32)
    sig = jax.nn.sigmoid(act)
    hidden = (act * sig).astype(jnp.bfloat16)
    expert_out = jnp.einsum("gsf,fd->gsd", hidden, down_mat, preferred_element_type=jnp.float32)
    dy_wide = rows_dy.astype(jnp.float32)
    gate_term = jnp.sum(dy_wide * expert_out, axis=2)
    local_col = jnp.sum(gate_term[:, :, None] * rows_x.astype(jnp.float32), axis=(0, 1))
    router_grads = dp_sum(local_col) / jnp.float32(column_tok)
    scaled = (rows_gate.astype(jnp.float32)[:, :, None] * dy_wide).astype(jnp.bfloat16)
    back = jnp.einsum("gsd,fd->gsf", scaled, down_mat, preferred_element_type=jnp.float32)
    act_grad = (back * sig * (1.0 + act * (1.0 - sig))).astype(jnp.bfloat16)
    route_grad = jnp.einsum(
        "gsf,df->gsd", act_grad, up_mat, preferred_element_type=jnp.float32
    ).astype(jnp.bfloat16)
    gate_back = jnp.broadcast_to(gate_term.astype(jnp.bfloat16)[:, :, None], (owners, most, 128))
    returned = lax.all_to_all(
        jnp.concatenate([route_grad, gate_back], axis=2), "expert", 0, 0, tiled=True
    )
    back_rows = returned[:, :, :width]
    back_gate = returned[:, :, width].astype(jnp.float32)
    token_grads = jnp.einsum(
        "cst,csd->td", pick, back_rows, preferred_element_type=jnp.float32
    ).astype(jnp.bfloat16)
    gate_back_tc = jnp.einsum(
        "cst,cs->tc", pick.astype(jnp.float32), back_gate, preferred_element_type=jnp.float32
    )
    gate_grads = jnp.sum(hit_f * gate_back_tc[:, None, :], axis=2).astype(jnp.bfloat16)
    return (token_grads, gate_grads, router_grads[None])


def solution(mesh):
    return jax.shard_map(
        body,
        mesh=mesh,
        in_specs=(
            P(("dp", "expert"), None),
            P(("dp", "expert"), None),
            P(("dp", "expert"), None),
            P(("dp", "expert"), None),
            P("expert", None, None),
            P("expert", None, None),
        ),
        out_specs=(P(("dp", "expert"), None), P(("dp", "expert"), None), P("expert", None)),
        check_vma=False,
    )
```

time: 172 us -> 157 us (0.913)
  starting transfers between devices: 89.2 us -> 39.3 us
  blocking collectives: 0 us -> 35.3 us
  waiting for transfers between devices: 32.6 us -> 54.1 us
  local copies, waits for them, and re-layouts: 19.4 us -> 9.23 us
  matrix products: 18.2 us -> 12.2 us
  other arithmetic: 10.3 us -> 5.2 us
    ppermute x6 -> x0, starting transfers between devices: 49.1 us -> none  [router_total(): acc = acc + lax.ppermute(acc, 'dp', perm)]
    all_to_all x5 -> x3, waiting for transfers between devices: 17.2 us -> 54.1 us  [the longest x1 21 us: dp_sum(): return lax.all_to_all(spread, 'dp', 0, 0, tiled=True).reshape(width)]
    all_to_all x0 -> x1, blocking collectives: none -> 35.3 us  [body(): recv = lax.all_to_all(packed, 'expert', 0, 0, tiled=True)]
    ppermute x6 -> x0, waiting for transfers between devices: 15.4 us -> none  [router_total(): acc = acc + lax.ppermute(acc, 'dp', perm)]
    reshape x9 -> x0, local copies, waits for them, and re-layouts: 11.3 us -> none  [the longest x1 2.19 us: body(): route_grad.reshape(groups, count, width)]
    dot_general x8 -> x9, matrix products: 18.2 us -> 12.2 us  [the longest x1 5.65 us: body(): jnp.einsum('gsf,df->gsd', act_grad, up_mat, preferred_element_type=jnp.fl...]
    convert_element_type x3 -> x0, local copies, waits for them, and re-layouts: 5.21 us -> none  [the longest x1 2.35 us: scale_part(): dy_wide = rows_dy.astype(jnp.float32)]
    another operation x3 -> x0, other arithmetic: 4.64 us -> none
  transfers between devices with their start and end apart: 11 -> 3, of which waited for: 9 -> 3; matrix products, arithmetic and copies ran while one was open for 14% -> 6% of each run, Pallas kernels for 0% -> 0%
where the time goes in v2:
time: 157 us; the launch traced here: 156 us
  waiting for transfers between devices  54.1 us (34%)
  starting transfers between devices  39.3 us (25%)
  blocking collectives  35.3 us (22%)
  matrix products  12.2 us (8%)
  local copies, waits for them, and re-layouts  9.23 us (6%)
  other arithmetic  5.2 us (3%)
    all_to_all x1, blocking collectives, body(): recv = lax.all_to_all(packed, 'expert', 0, 0, tiled=True)  35.3 us
    all_to_all x1, starting transfers between devices, dp_sum(): mine = jnp.sum(lax.all_to_all(parts, 'dp', 0, 0, tiled=True), axis=0)  29.1 us
    all_to_all x1, waiting for transfers between devices, dp_sum(): return lax.all_to_all(spread, 'dp', 0, 0, tiled=True).reshape(width)  21 us
    all_to_all x1, waiting for transfers between devices, dp_sum(): mine = jnp.sum(lax.all_to_all(parts, 'dp', 0, 0, tiled=True), axis=0)  17.9 us
    all_to_all x1, waiting for transfers between devices, body(): lax.all_to_all(jnp.concatenate([route_grad, gate_back], axis=2), 'expert'...  15.2 us
    dot_general x1, matrix products, body(): jnp.einsum('gsf,df->gsd', act_grad, up_mat, preferred_element_type=jnp.fl...  5.65 us
    all_to_all x1, starting transfers between devices, body(): lax.all_to_all(jnp.concatenate([route_grad, gate_back], axis=2), 'expert'...  5.57 us
    all_to_all x1, starting transfers between devices, dp_sum(): return lax.all_to_all(spread, 'dp', 0, 0, tiled=True).reshape(width)  4.59 us
  transfers between devices with their start and end apart: 3, of which 3 were waited for; matrix products, arithmetic and copies ran while one was open for 6% of the time, Pallas kernels for 0%

profile of v2, /device:TPU:2, one launch (start us, length us, event | category | flops | bytes accessed | tf_op | source)
XLA Modules:
  0.0 156.1 jit_solution(12295810978316446157)
XLA Ops:
  0.6 0.0 copy-start
  0.6 0.9 fusion.52
  1.5 0.8 add_select_fusion.1
  2.3 0.7 convert_element_type.46
  3.0 0.1 fusion.51
  3.2 0.1 fusion.46
  3.3 0.1 copy.41
  3.4 0.0 copy-start.4
  3.4 1.4 convolution_convert_fusion.1
  4.9 0.0 copy-done.4
  4.9 0.3 convolution_convert_fusion
  5.2 0.1 broadcast_in_dim.6
  5.3 0.1 pad_maximum_fusion
  5.4 0.3 copy.30
  5.7 35.3 %all_to_all.25 = bf16[16,10,4224]{2,1,0:T(8,128)(2,1)S(1)} all-to-all(bf16[16,10,4224]{2,1,0:T(8,128)(2,1)S(1)} %copy.30), channel_id=1, replica_groups=mesh['dp'=64,'expert'=16] {'expert'}, dimensions={0} | all-to-all | bytes 2703360 | tf_op jit(solution)/shard_map/all_to_all | solution.py:52
  41.0 0.0 copy-start.1
  41.0 1.3 copy-done.1
  42.4 0.2 copy.44
  42.6 0.1 copy.32
  42.7 0.0 copy-start.2
  42.7 1.8 %fusion.60 = (bf16[16,10,2048]{2,1,0:T(8,128)(2,1)S(1)}, bf16[16,10,2048]{2,1,0:T(8,128)(2,1)S(1)}) fusion(bf16[16,10,4224]{2,1,0:T(8,128)(2,1)} %copy-done.1), kind=kLoop, calls=%fused_computation.65 | loop fusion | bytes 2621440 | tf_op jit(solution)/shard_map/slice | solution.py:53
  44.5 0.0 copy-start.3
  44.5 0.7 copy-done.2
  45.2 1.1 fusion.3
  46.3 0.0 copy-start.5
  46.3 0.0 copy-done.3
  46.3 0.0 copy-done
  46.3 1.0 fusion.61
  47.3 0.0 copy-done.5
  47.3 0.8 fusion.62
  48.1 0.7 all_to_all.18
  48.8 29.1 %all-to-all-start.2 = ((f32[64,1,32]{2,1,0:T(1,128)}), f32[64,1,32]{2,1,0:T(1,128)S(1)}, u32[]{:S(2)}, u32[]{:S(2)}) async-start(f32[64,1,32]{2,1,0:T(1,128)} %bitcast.16), calls=%async_computation.2 | async-start | bytes 65536 | tf_op jit(solution)/shard_map/all_to_all | solution.py:15
  77.9 5.7 %fusion.13 = bf16[16,10,2048]{2,0,1:T(8,128)(2,1)} fusion(bf16[1,2048,768]{2,1,0:T(8,128)(2,1)} %param.10, bf16[1,768,2048]{2,1,0:T(8,128)(2,1)S(1)} %copy-done, f32[16,10]{0,1:T(8,128)S(1)} %copy.32, f32[16,10,768]{2,0,1:T(8,128)} %copy-done.5, bf16[16,10,2048]{2,1,0:T(8,128)(2,1)} %copy-done.3), kind=kOutput, calls=%fused_computation.12 | convolution fusion | flops 1009049600 | bytes 8094336 | tf_op jit(solution)/shard_map/gsf,df->gsd/dot_general | solution.py:67
  83.5 17.9 %all-to-all-done.2 = f32[64,1,32]{2,1,0:T(1,128)S(1)} async-done(((f32[64,1,32]{2,1,0:T(1,128)}), f32[64,1,32]{2,1,0:T(1,128)S(1)}, u32[]{:S(2)}, u32[]{:S(2)}) %all-to-all-start.2) | async-done | bytes 8224 | tf_op jit(solution)/shard_map/all_to_all | solution.py:15
  101.4 0.1 reduce_sum.59
  101.5 0.6 broadcast_in_dim.8
  102.1 4.6 %all-to-all-start.3 = ((f32[64,1,32]{2,1,0:T(1,128)}), f32[64,1,32]{2,1,0:T(1,128)S(1)}, u32[]{:S(2)}, u32[]{:S(2)}) async-start(f32[64,1,32]{2,1,0:T(1,128)} %broadcast_in_dim.8), calls=%async_computation.3 | async-start | bytes 65536 | tf_op jit(solution)/shard_map/all_to_all | solution.py:17
  106.7 0.1 broadcast_in_dim.7
  106.8 1.1 pad_maximum_fusion.1
  108.0 1.2 copy.35
  109.2 21.0 %all-to-all-done.3 = f32[64,1,32]{2,1,0:T(1,128)S(1)} async-done(((f32[64,1,32]{2,1,0:T(1,128)}), f32[64,1,32]{2,1,0:T(1,128)S(1)}, u32[]{:S(2)}, u32[]{:S(2)}) %all-to-all-start.3) | async-done | bytes 8224 | tf_op jit(solution)/shard_map/all_to_all | solution.py:17
  130.2 5.6 %all-to-all-start.1 = ((bf16[16,10,2176]{2,1,0:T(8,128)(2,1)}), bf16[16,10,2176]{2,1,0:T(8,128)(2,1)}, u32[]{:S(2)}, u32[]{:S(2)}) async-start(bf16[16,10,2176]{2,1,0:T(8,128)(2,1)} %copy.35), calls=%async_computation.1 | async-start | bytes 2228224 | tf_op jit(solution)/shard_map/all_to_all | solution.py:71
  135.8 0.1 multiply_reduce_fusion
  135.9 0.7 div.30
  136.6 15.2 %all-to-all-done.1 = bf16[16,10,2176]{2,1,0:T(8,128)(2,1)} async-done(((bf16[16,10,2176]{2,1,0:T(8,128)(2,1)}), bf16[16,10,2176]{2,1,0:T(8,128)(2,1)}, u32[]{:S(2)}, u32[]{:S(2)}) %all-to-all-start.1) | async-done | bytes 696352 | tf_op jit(solution)/shard_map/all_to_all | solution.py:71
  151.8 1.3 slice.23
  153.1 1.3 fusion.16
  154.4 1.0 fusion.44
  155.4 0.6 select_reduce_fusion
  (5 shorter events, 0.1 us)
Async XLA Ops:
  0.6 45.7 %copy-start = (bf16[1,768,2048]{2,1,0:T(8,128)(2,1)S(1)}, bf16[1,768,2048]{2,1,0:T(8,128)(2,1)}, u32[]{:S(2)}) copy-start(bf16[1,768,2048]{2,1,0:T(8,128)(2,1)} %param.11) | copy-start | bytes 9437188
  3.4 1.5 copy-start.4
  41.0 1.4 copy-start.1
  42.7 2.5 %copy-start.2 = (bf16[1,2048,768]{2,1,0:T(8,128)(2,1)S(1)}, bf16[1,2048,768]{2,1,0:T(8,128)(2,1)}, u32[]{:S(2)}) copy-start(bf16[1,2048,768]{2,1,0:T(8,128)(2,1)} %param.10) | copy-start | bytes 9437188
  44.5 1.8 %copy-start.3 = (bf16[16,10,2048]{2,1,0:T(8,128)(2,1)}, bf16[16,10,2048]{2,1,0:T(8,128)(2,1)S(1)}, u32[]{:S(2)}) copy-start(bf16[16,10,2048]{2,1,0:T(8,128)(2,1)S(1)} %get-tuple-element.6) | copy-start | bytes 1966084
  46.3 1.1 copy-start.5
  48.8 52.6 %all-to-all-start.2 = ((f32[64,1,32]{2,1,0:T(1,128)}), f32[64,1,32]{2,1,0:T(1,128)S(1)}, u32[]{:S(2)}, u32[]{:S(2)}) async-start(f32[64,1,32]{2,1,0:T(1,128)} %bitcast.16), calls=%async_computation.2 | async-start | bytes 65536 | tf_op jit(solution)/shard_map/all_to_all | solution.py:15
  102.1 28.1 %all-to-all-start.3 = ((f32[64,1,32]{2,1,0:T(1,128)}), f32[64,1,32]{2,1,0:T(1,128)S(1)}, u32[]{:S(2)}, u32[]{:S(2)}) async-start(f32[64,1,32]{2,1,0:T(1,128)} %broadcast_in_dim.8), calls=%async_computation.3 | async-start | bytes 65536 | tf_op jit(solution)/shard_map/all_to_all | solution.py:17
  130.2 21.6 %all-to-all-start.1 = ((bf16[16,10,2176]{2,1,0:T(8,128)(2,1)}), bf16[16,10,2176]{2,1,0:T(8,128)(2,1)}, u32[]{:S(2)}, u32[]{:S(2)}) async-start(bf16[16,10,2176]{2,1,0:T(8,128)(2,1)} %copy.35), calls=%async_computation.1 | async-start | bytes 2228224 | tf_op jit(solution)/shard_map/all_to_all | solution.py:71

commit v3 on v2

--- a/solution.py
+++ b/solution.py
@@ -4,12 +4,15 @@
 from jax.sharding import PartitionSpec as P
 
 EXP_DEV = 8
-DP_REDUCE = "a2a"
+DP_REDUCE = "sc"
 
 
 def dp_sum(local_col):
     n = lax.axis_size("dp")
     width = local_col.shape[0]
+    if DP_REDUCE == "sc":
+        b = jnp.broadcast_to(local_col, (16, width)) * (jnp.arange(16) == 0).astype(jnp.float32)[:, None]
+        return jnp.sum(lax.psum(b, "dp"), axis=0)
     if DP_REDUCE == "a2a":
         parts = local_col.reshape(n, width // n)
         mine = jnp.sum(lax.all_to_all(parts, "dp", 0, 0, tiled=True), axis=0)

time: 157 us -> 472 us (3.01)
  the two profiles are of different devices: /device:TPU:2 before, /device:TPU:1 now
where the time goes in v3:
time: 472 us
  waiting for transfers between devices  415 us (88%)
  between operations  14.2 us (3%)
  matrix products  13.1 us (3%)
  starting transfers between devices  12.1 us (3%)
  local copies, waits for them, and re-layouts  8.81 us (2%)
  other arithmetic  7.89 us (2%)
    psum x1, waiting for transfers between devices, dp_sum(): return jnp.sum(lax.psum(b, 'dp'), axis=0)  392 us
    all_to_all x1, waiting for transfers between devices, body(): recv = lax.all_to_all(packed, 'expert', 0, 0, tiled=True)  23.6 us
  transfers between devices with their start and end apart: 3, of which 2 were waited for; matrix products, arithmetic and copies ran while one was open for 0% of the time, Pallas kernels for 0%

profile of v3, /device:TPU:1, one launch (start us, length us, event | category | flops | bytes accessed | tf_op | source)
XLA Modules:
  0.0 471.5 jit_solution(17987282489176383409)
XLA Ops:
  7.2 0.0 copy-start
  7.2 0.9 fusion.52
  8.0 0.8 add_select_fusion.1
  8.8 0.7 convert_element_type.53
  9.5 0.1 fusion.51
  9.7 0.1 fusion.46
  9.9 0.1 copy.39
  10.0 0.0 copy-start.5
  10.0 1.4 convolution_convert_fusion.1
  11.4 0.0 copy-done.5
  11.4 0.3 convolution_convert_fusion
  11.8 0.1 broadcast_in_dim.6
  11.8 0.1 pad_maximum_fusion
  12.0 1.6 copy.29
  13.6 7.6 %all-to-all-start = ((bf16[16,10,4224]{2,1,0:T(8,128)(2,1)}), bf16[16,10,4224]{2,1,0:T(8,128)(2,1)}, u32[]{:S(2)}, u32[]{:S(2)}) async-start(bf16[16,10,4224]{2,1,0:T(8,128)(2,1)} %copy.29), calls=%async_computation | async-start | bytes 4325376 | tf_op jit(solution)/shard_map/all_to_all | solution.py:55
  21.2 23.6 %all-to-all-done = bf16[16,10,4224]{2,1,0:T(8,128)(2,1)} async-done(((bf16[16,10,4224]{2,1,0:T(8,128)(2,1)}), bf16[16,10,4224]{2,1,0:T(8,128)(2,1)}, u32[]{:S(2)}, u32[]{:S(2)}) %all-to-all-start) | async-done | bytes 1351712 | tf_op jit(solution)/shard_map/all_to_all | solution.py:55
  44.8 0.8 slice.20
  45.7 0.2 copy.42
  45.9 0.1 copy.31
  46.0 0.0 copy-start.1
  46.0 1.8 fusion.60
  47.8 0.0 copy-start.2
  47.8 0.0 copy-start.3
  47.8 0.7 copy-done.1
  48.5 1.1 fusion.3
  49.6 0.0 copy-done.2
  49.6 0.0 copy-start.6
  49.6 0.0 copy-done.3
  49.6 0.8 copy-done.6
  50.4 0.0 copy-done
  50.4 2.0 fusion.61
  52.4 5.6 %fusion.13 = bf16[16,10,2048]{2,0,1:T(8,128)(2,1)} fusion(bf16[1,2048,768]{2,1,0:T(8,128)(2,1)} %param.10, bf16[1,768,2048]{2,1,0:T(8,128)(2,1)S(1)} %copy-done, f32[16,10]{0,1:T(8,128)S(1)} %copy.31, f32[16,10,768]{2,0,1:T(8,128)} %copy-done.6, bf16[16,10,2048]{2,1,0:T(8,128)(2,1)} %copy-done.3), kind=kOutput, calls=%fused_computation.12 | convolution fusion | flops 1009049600 | bytes 8094336 | tf_op jit(solution)/shard_map/gsf,df->gsd/dot_general | solution.py:70
  58.0 0.0 copy-start.4
  58.0 2.4 fusion.62
  60.4 0.1 broadcast_in_dim.7
  60.5 0.0 copy-done.4
  60.5 0.1 pad_maximum_fusion.1
  60.6 1.2 copy.34
  61.8 4.4 all-to-all-start.1
  66.3 0.0 all-reduce.2.cloned.1.call-start
  66.3 0.7 broadcast_multiply_fusion
  67.1 0.0 all-reduce.2.cloned.1.call-update
  67.1 391.7 %all-reduce.2.cloned.1.call-done = f32[16,2048]{1,0:T(8,128)} async-done(((f32[16,2048]{1,0:T(8,128)}), f32[16,2048]{1,0:T(8,128)}) %all-reduce.2.cloned.1.call-update) | async-done | bytes 131088 | tf_op jit(solution)/shard_map/psum | solution.py:15
  458.8 0.9 reduce_sum.59
  459.8 0.6 broadcast_multiply_fusion.1
  460.4 0.0 all-to-all-done.1
  460.4 1.3 slice.23
  461.7 1.3 fusion.16
  463.0 1.0 fusion.44
  464.0 0.6 select_reduce_fusion
  (5 shorter events, 0.1 us)
Async XLA Ops:
  7.2 43.2 %copy-start = (bf16[1,768,2048]{2,1,0:T(8,128)(2,1)S(1)}, bf16[1,768,2048]{2,1,0:T(8,128)(2,1)}, u32[]{:S(2)}) copy-start(bf16[1,768,2048]{2,1,0:T(8,128)(2,1)} %param.11) | copy-start | bytes 9437188
  10.0 1.5 copy-start.5
  13.6 31.2 %all-to-all-start = ((bf16[16,10,4224]{2,1,0:T(8,128)(2,1)}), bf16[16,10,4224]{2,1,0:T(8,128)(2,1)}, u32[]{:S(2)}, u32[]{:S(2)}) async-start(bf16[16,10,4224]{2,1,0:T(8,128)(2,1)} %copy.29), calls=%async_computation | async-start | bytes 4325376 | tf_op jit(solution)/shard_map/all_to_all | solution.py:55
  46.0 2.5 copy-start.1
  47.8 1.8 copy-start.2
  47.8 1.8 copy-start.3
  49.6 0.8 copy-start.6
  58.0 2.5 copy-start.4
  61.8 398.5 %all-to-all-start.1 = ((bf16[16,10,2176]{2,1,0:T(8,128)(2,1)}), bf16[16,10,2176]{2,1,0:T(8,128)(2,1)}, u32[]{:S(2)}, u32[]{:S(2)}) async-start(bf16[16,10,2176]{2,1,0:T(8,128)(2,1)} %copy.34), calls=%async_computation.1 | async-start | bytes 2228224 | tf_op jit(solution)/shard_map/all_to_all | solution.py:74
  66.3 392.5 %all-reduce.2.cloned.1.call-start = ((), (), s32[]{:S(2)}) async-start(), calls=%async_computation.2 | async-start | bytes 262144 | tf_op jit(solution)/shard_map/psum | solution.py:15
Sparse Core Ops, SparseCore 0:
  70.0 388.7 all-reduce.1

commit v4 on v2

--- a/solution.py
+++ b/solution.py
@@ -1,26 +1,13 @@
 import jax
 import jax.numpy as jnp
 from jax import lax
-from jax.sharding import PartitionSpec as P
+from jax.sharding import Mesh, PartitionSpec as P
 
 EXP_DEV = 8
-DP_REDUCE = "a2a"
 
 
 def dp_sum(local_col):
-    n = lax.axis_size("dp")
-    width = local_col.shape[0]
-    if DP_REDUCE == "a2a":
-        parts = local_col.reshape(n, width // n)
-        mine = jnp.sum(lax.all_to_all(parts, "dp", 0, 0, tiled=True), axis=0)
-        spread = jnp.broadcast_to(mine[None], (n, width // n))
-        return lax.all_to_all(spread, "dp", 0, 0, tiled=True).reshape(width)
-    acc = local_col
-    d = 1
-    while d < n:
-        acc = acc + lax.ppermute(acc, "dp", [(i, i ^ d) for i in range(n)])
-        d *= 2
-    return acc
+    return lax.psum(lax.psum(lax.psum(local_col, "core"), "near"), "far")
 
 
 def body(tokens, upstream, expert_ids, gate_weights, w_up, w_down):
@@ -28,7 +15,7 @@
     experts = EXP_DEV * owners
     tok_count, top = expert_ids.shape
     width = tokens.shape[1]
-    column_tok = tok_count * lax.axis_size("dp")
+    column_tok = tok_count * lax.axis_size(("far", "near", "core"))
     most = tok_count * top // experts + tok_count * top // (4 * experts)
     up_mat = w_up[0]
     down_mat = w_down[0]
@@ -84,17 +71,22 @@
 
 
 def solution(mesh):
+    n_dp = mesh.shape["dp"]
+    rows = ("far", "near", "core", "expert")
+    split = Mesh(
+        mesh.devices.reshape(n_dp // 8, 4, 2, mesh.shape["expert"]), rows
+    )
     return jax.shard_map(
         body,
-        mesh=mesh,
+        mesh=split,
         in_specs=(
-            P(("dp", "expert"), None),
-            P(("dp", "expert"), None),
-            P(("dp", "expert"), None),
-            P(("dp", "expert"), None),
+            P(rows, None),
+            P(rows, None),
+            P(rows, None),
+            P(rows, None),
             P("expert", None, None),
             P("expert", None, None),
         ),
-        out_specs=(P(("dp", "expert"), None), P(("dp", "expert"), None), P("expert", None)),
+        out_specs=(P(rows, None), P(rows, None), P("expert", None)),
         check_vma=False,
     )

time: 157 us -> 122 us (0.78)
  the two profiles are of different devices: /device:TPU:2 before, /device:TPU:4 now
where the time goes in v4:
time: 122 us
  blocking collectives  86.3 us (71%)
  matrix products  13.1 us (11%)
  local copies, waits for them, and re-layouts  7.94 us (7%)
  other arithmetic  7.24 us (6%)
  starting transfers between devices  6.3 us (5%)
    psum x3, blocking collectives, dp_sum(): return lax.psum(lax.psum(lax.psum(local_col, 'core'), 'near'), 'far')  51.8 us
    all_to_all x1, blocking collectives, body(): recv = lax.all_to_all(packed, 'expert', 0, 0, tiled=True)  34.5 us
    all_to_all x1, starting transfers between devices, body(): lax.all_to_all(jnp.concatenate([route_grad, gate_back], axis=2), 'expert'...  6.3 us
    dot_general x1, matrix products, body(): jnp.einsum('gsf,df->gsd', act_grad, up_mat, preferred_element_type=jnp.fl...  5.62 us
    unnamed x15, local copies, waits for them, and re-layouts  3.02 us
  transfers between devices with their start and end apart: 1, of which 0 were waited for; matrix products, arithmetic and copies ran while one was open for 2% of the time, Pallas kernels for 0%

profile of v4, /device:TPU:4, one launch (start us, length us, event | category | flops | bytes accessed | tf_op | source)
XLA Modules:
  0.0 121.7 jit_solution(17728531810281446327)
XLA Ops:
  0.6 0.0 copy-start
  0.6 0.9 fusion.52
  1.5 0.8 add_select_fusion.1
  2.3 0.7 convert_element_type.46
  3.0 0.1 fusion.51
  3.2 0.1 fusion.46
  3.3 0.1 copy.39
  3.4 0.0 copy-start.5
  3.4 1.4 %convolution_convert_fusion.1 = bf16[16,10,2048]{2,0,1:T(8,128)(2,1)S(1)} fusion(bf16[128,2048]{1,0:T(8,128)(2,1)} %param.6, f32[16,128]{1,0:T(8,128)S(1)} %fusion.51, pred[16,128]{1,0:T(8,128)(4,1)S(1)} %compare_bitcast_fusion), kind=kOutput, calls=%fused_computation.14 | convolution fusion | flops 84254720 | bytes 1189888 | tf_op jit(solution)/shard_map/cst,td->csd/dot_general | solution.py:32
  4.9 0.0 copy-done.5
  4.9 0.3 convolution_convert_fusion
  5.2 0.1 broadcast_in_dim.6
  5.3 0.1 pad_maximum_fusion
  5.4 0.3 copy.29
  5.7 34.5 %all_to_all.10 = bf16[16,10,4224]{2,1,0:T(8,128)(2,1)S(1)} all-to-all(bf16[16,10,4224]{2,1,0:T(8,128)(2,1)S(1)} %copy.29), channel_id=1, replica_groups=mesh['far'=8,'near'=4,'core'=2,'expert'=16] {'expert'}, dimensions={0} | all-to-all | bytes 2703360 | tf_op jit(solution)/shard_map/all_to_all | solution.py:39
  40.2 0.0 copy-start.1
  40.2 1.3 %copy-done.1 = bf16[16,10,4224]{2,1,0:T(8,128)(2,1)} copy-done((bf16[16,10,4224]{2,1,0:T(8,128)(2,1)}, bf16[16,10,4224]{2,1,0:T(8,128)(2,1)S(1)}, u32[]{:S(2)}) %copy-start.1) | copy-done | bytes 1351704
  41.6 0.2 copy.42
  41.8 0.1 copy.31
  41.9 0.0 copy-start.2
  41.9 1.8 %fusion.60 = (bf16[16,10,2048]{2,1,0:T(8,128)(2,1)S(1)}, bf16[16,10,2048]{2,1,0:T(8,128)(2,1)S(1)}) fusion(bf16[16,10,4224]{2,1,0:T(8,128)(2,1)} %copy-done.1), kind=kLoop, calls=%fused_computation.65 | loop fusion | bytes 2621440 | tf_op jit(solution)/shard_map/slice | solution.py:40
  43.7 0.0 copy-start.3
  43.7 0.0 copy-start.4
  43.7 0.7 copy-done.2
  44.4 1.1 fusion.3
  45.5 0.0 copy-done.3
  45.5 0.0 copy-start.6
  45.5 0.0 copy-done.4
  45.5 0.8 copy-done.6
  46.3 0.0 copy-done
  46.3 2.0 %fusion.61 = (bf16[16,10]{0,1:T(8,128)(2,1)S(1)}, f32[16,10,2048]{2,0,1:T(8,128)}) fusion(bf16[1,768,2048]{2,1,0:T(8,128)(2,1)S(1)} %copy-done, f32[16,10,768]{2,0,1:T(8,128)S(1)} %fusion.3, bf16[16,10,2048]{2,1,0:T(8,128)(2,1)S(1)} %get-tuple-element.6), kind=kOutput, calls=%fused_computation.66 | convolution fusion | flops 504913760 | bytes 5603648 | tf_op jit(solution)/shard_map/gsf,fd->gsd/dot_general | solution.py:46
  48.3 5.6 %fusion.13 = bf16[16,10,2048]{2,0,1:T(8,128)(2,1)} fusion(bf16[1,2048,768]{2,1,0:T(8,128)(2,1)} %param.10, bf16[1,768,2048]{2,1,0:T(8,128)(2,1)S(1)} %copy-done, f32[16,10]{0,1:T(8,128)S(1)} %copy.31, f32[16,10,768]{2,0,1:T(8,128)} %copy-done.6, bf16[16,10,2048]{2,1,0:T(8,128)(2,1)} %copy-done.4), kind=kOutput, calls=%fused_computation.12 | convolution fusion | flops 1009049600 | bytes 8094336 | tf_op jit(solution)/shard_map/gsf,df->gsd/dot_general | solution.py:54
  53.9 0.1 broadcast_in_dim.7
  54.0 1.1 pad_maximum_fusion.1
  55.1 1.2 copy.34
  56.3 6.3 %all-to-all-start.1 = ((bf16[16,10,2176]{2,1,0:T(8,128)(2,1)}), bf16[16,10,2176]{2,1,0:T(8,128)(2,1)}, u32[]{:S(2)}, u32[]{:S(2)}) async-start(bf16[16,10,2176]{2,1,0:T(8,128)(2,1)} %copy.34), calls=%async_computation.1 | async-start | bytes 2228224 | tf_op jit(solution)/shard_map/all_to_all | solution.py:58
  62.6 2.4 %fusion.62 = f32[2048]{0:T(1024)S(1)} fusion(bf16[16,10,2048]{2,1,0:T(8,128)(2,1)} %copy-done.3, f32[16,10,2048]{2,0,1:T(8,128)} %get-tuple-element.8), kind=kOutput, calls=%fused_computation.67 | output fusion | flops 983199 | bytes 1974272 | tf_op jit(solution)/shard_map/mul | solution.py:49
  65.0 2.5 %psum.21 = f32[2048]{0:T(1024)S(1)} all-reduce(f32[2048]{0:T(1024)S(1)} %fusion.62), channel_id=1, replica_groups=mesh['far'=8,'near'=4,'core'=2,'expert'=16] {'core'}, use_global_device_ids=true, to_apply=%region_5.6 | all-reduce | flops 2048 | bytes 16384 | tf_op jit(solution)/shard_map/psum | solution.py:10
  67.5 12.9 %psum.22 = f32[2048]{0:T(1024)S(1)} all-reduce(f32[2048]{0:T(1024)S(1)} %psum.21), channel_id=1, replica_groups=mesh['far'=8,'near'=4,'core'=2,'expert'=16] {'near'}, use_global_device_ids=true, to_apply=%region_6.7 | all-reduce | flops 2048 | bytes 16384 | tf_op jit(solution)/shard_map/psum | solution.py:10
  80.4 36.4 %psum.23 = f32[2048]{0:T(1024)S(1)} all-reduce(f32[2048]{0:T(1024)S(1)} %psum.22), channel_id=1, replica_groups=mesh['far'=8,'near'=4,'core'=2,'expert'=16] {'far'}, use_global_device_ids=true, to_apply=%region_7.8 | all-reduce | flops 2048 | bytes 16384 | tf_op jit(solution)/shard_map/psum | solution.py:10
  116.8 0.6 broadcast_multiply_fusion
  117.4 0.0 all-to-all-done.1
  117.4 1.3 %slice.23 = bf16[16,10,2048]{2,1,0:T(8,128)(2,1)S(1)} slice(bf16[16,10,2176]{2,1,0:T(8,128)(2,1)} %all-to-all-done.1), slice={[0:16], [0:10], [0:2048]} | slice | bytes 1310720 | tf_op jit(solution)/shard_map/slice | solution.py:61
  118.7 1.3 %fusion.16 = bf16[128,2048]{1,0:T(8,128)(2,1)} fusion(bf16[16,10,2048]{2,1,0:T(8,128)(2,1)S(1)} %slice.23, f32[16,128]{1,0:T(8,128)S(1)} %fusion.51, pred[16,128]{1,0:T(8,128)(4,1)S(1)} %compare_bitcast_fusion), kind=kOutput, calls=%fused_computation.15 | convolution fusion | flops 84189184 | bytes 1189888 | tf_op jit(solution)/shard_map/cst,csd->td/dot_general | solution.py:63
  120.1 1.0 fusion.44
  121.1 0.6 select_reduce_fusion
  (5 shorter events, 0.1 us)
Async XLA Ops:
  0.6 45.7 %copy-start = (bf16[1,768,2048]{2,1,0:T(8,128)(2,1)S(1)}, bf16[1,768,2048]{2,1,0:T(8,128)(2,1)}, u32[]{:S(2)}) copy-start(bf16[1,768,2048]{2,1,0:T(8,128)(2,1)} %param.11) | copy-start | bytes 9437188
  3.4 1.5 %copy-start.5 = (bf16[128,2048]{1,0:T(8,128)(2,1)S(1)}, bf16[128,2048]{1,0:T(8,128)(2,1)}, u32[]{:S(2)}) copy-start(bf16[128,2048]{1,0:T(8,128)(2,1)} %param.7) | copy-start | bytes 1572868
  40.2 1.4 %copy-start.1 = (bf16[16,10,4224]{2,1,0:T(8,128)(2,1)}, bf16[16,10,4224]{2,1,0:T(8,128)(2,1)S(1)}, u32[]{:S(2)}) copy-start(bf16[16,10,4224]{2,1,0:T(8,128)(2,1)S(1)} %all_to_all.10) | copy-start | bytes 4055044
  41.9 2.5 %copy-start.2 = (bf16[1,2048,768]{2,1,0:T(8,128)(2,1)S(1)}, bf16[1,2048,768]{2,1,0:T(8,128)(2,1)}, u32[]{:S(2)}) copy-start(bf16[1,2048,768]{2,1,0:T(8,128)(2,1)} %param.10) | copy-start | bytes 9437188
  43.7 1.8 %copy-start.3 = (bf16[16,10,2048]{2,1,0:T(8,128)(2,1)}, bf16[16,10,2048]{2,1,0:T(8,128)(2,1)S(1)}, u32[]{:S(2)}) copy-start(bf16[16,10,2048]{2,1,0:T(8,128)(2,1)S(1)} %get-tuple-element.5) | copy-start | bytes 1966084
  43.7 1.8 %copy-start.4 = (bf16[16,10,2048]{2,1,0:T(8,128)(2,1)}, bf16[16,10,2048]{2,1,0:T(8,128)(2,1)S(1)}, u32[]{:S(2)}) copy-start(bf16[16,10,2048]{2,1,0:T(8,128)(2,1)S(1)} %get-tuple-element.6) | copy-start | bytes 1966084
  45.5 0.8 copy-start.6
  56.3 61.1 %all-to-all-start.1 = ((bf16[16,10,2176]{2,1,0:T(8,128)(2,1)}), bf16[16,10,2176]{2,1,0:T(8,128)(2,1)}, u32[]{:S(2)}, u32[]{:S(2)}) async-start(bf16[16,10,2176]{2,1,0:T(8,128)(2,1)} %copy.34), calls=%async_computation.1 | async-start | bytes 2228224 | tf_op jit(solution)/shard_map/all_to_all | solution.py:58

commit v5 on v4

--- a/solution.py
+++ b/solution.py
@@ -35,11 +35,11 @@
         "cst,tc->cs", pick.astype(jnp.float32), gate_tc, preferred_element_type=jnp.float32
     )
     gate_cols = jnp.broadcast_to(send_gate[:, :, None], (owners, most, 128))
-    packed = jnp.concatenate([send_x, send_dy, gate_cols], axis=2).astype(jnp.bfloat16)
+    packed = jnp.concatenate([send_dy, gate_cols], axis=2).astype(jnp.bfloat16)
+    rows_x = lax.all_to_all(send_x.astype(jnp.bfloat16), "expert", 0, 0, tiled=True)
     recv = lax.all_to_all(packed, "expert", 0, 0, tiled=True)
-    rows_x = recv[:, :, :width]
-    rows_dy = recv[:, :, width : 2 * width]
-    rows_gate = recv[:, :, 2 * width]
+    rows_dy = recv[:, :, :width]
+    rows_gate = recv[:, :, width]
     act = jnp.einsum("gsd,df->gsf", rows_x, up_mat, preferred_element_type=jnp.float32)
     sig = jax.nn.sigmoid(act)
     hidden = (act * sig).astype(jnp.bfloat16)

time: 122 us -> 131 us (1.074)
  the two profiles are of different devices: /device:TPU:4 before, /device:TPU:2 now
where the time goes in v5:
time: 131 us; the launch traced here: 130 us
  blocking collectives  48.4 us (37%)
  starting transfers between devices  28.7 us (22%)
  waiting for transfers between devices  19.5 us (15%)
  matrix products  17.5 us (13%)
  local copies, waits for them, and re-layouts  8.94 us (7%)
  other arithmetic  6.35 us (5%)
    psum x3, blocking collectives, dp_sum(): return lax.psum(lax.psum(lax.psum(local_col, 'core'), 'near'), 'far')  48.4 us
    all_to_all x1, starting transfers between devices, body(): lax.all_to_all(send_x.astype(jnp.bfloat16), 'expert', 0, 0, tiled=True)  17.2 us
    all_to_all x1, waiting for transfers between devices, body(): lax.all_to_all(send_x.astype(jnp.bfloat16), 'expert', 0, 0, tiled=True)  10 us
    all_to_all x1, waiting for transfers between devices, body(): recv = lax.all_to_all(packed, 'expert', 0, 0, tiled=True)  9.44 us
    dot_general x1, matrix products, body(): jnp.einsum('gsf,df->gsd', act_grad, up_mat, preferred_element_type=jnp.fl...  5.81 us
    all_to_all x1, starting transfers between devices, body(): recv = lax.all_to_all(packed, 'expert', 0, 0, tiled=True)  5.8 us
    all_to_all x1, starting transfers between devices, body(): lax.all_to_all(jnp.concatenate([route_grad, gate_back], axis=2), 'expert'...  5.67 us
    dot_general x1, matrix products, body(): jnp.einsum('gsf,fd->gsd', hidden, down_mat, preferred_element_type=jnp.fl...  3.16 us
  transfers between devices with their start and end apart: 3, of which 2 were waited for; matrix products, arithmetic and copies ran while one was open for 6% of the time, Pallas kernels for 0%

profile of v5, /device:TPU:2, one launch (start us, length us, event | category | flops | bytes accessed | tf_op | source)
XLA Modules:
  0.0 130.1 jit_solution(8539032767680625095)
XLA Ops:
  0.6 0.0 copy-start
  0.6 0.9 fusion.53
  1.5 0.8 add_select_fusion.1
  2.3 0.7 convert_element_type.49
  3.0 0.1 fusion.52
  3.2 1.4 %convolution_convert_fusion = bf16[16,10,2048]{2,0,1:T(8,128)(2,1)S(1)} fusion(bf16[128,2048]{1,0:T(8,128)(2,1)} %param.6, f32[16,128]{1,0:T(8,128)S(1)} %fusion.52, pred[16,128]{1,0:T(8,128)(4,1)S(1)} %compare_bitcast_fusion), kind=kOutput, calls=%fused_computation.11 | convolution fusion | flops 84254720 | bytes 1189888 | tf_op jit(solution)/shard_map/cst,td->csd/dot_general | solution.py:32
  4.5 1.4 %copy.35 = bf16[16,10,2048]{2,1,0:T(8,128)(2,1)} copy(bf16[16,10,2048]{2,0,1:T(8,128)(2,1)S(1)} %convolution_convert_fusion) | data formatting | bytes 1310720 | tf_op jit(solution)/shard_map/convert_element_type | solution.py:39
  6.0 17.2 %all-to-all-start.1 = ((bf16[16,10,2048]{2,1,0:T(8,128)(2,1)}), bf16[16,10,2048]{2,1,0:T(8,128)(2,1)}, u32[]{:S(2)}, u32[]{:S(2)}) async-start(bf16[16,10,2048]{2,1,0:T(8,128)(2,1)} %copy.35), calls=%async_computation.1 | async-start | bytes 2097152 | tf_op jit(solution)/shard_map/all_to_all | solution.py:39
  23.2 0.1 fusion.47
  23.3 0.1 copy.45
  23.4 1.4 %convolution_convert_fusion.1 = bf16[16,10,2048]{2,0,1:T(8,128)(2,1)S(1)} fusion(bf16[128,2048]{1,0:T(8,128)(2,1)} %param.7, f32[16,128]{1,0:T(8,128)S(1)} %fusion.52, pred[16,128]{1,0:T(8,128)(4,1)S(1)} %compare_bitcast_fusion), kind=kOutput, calls=%fused_computation.12 | convolution fusion | flops 84254720 | bytes 1189888 | tf_op jit(solution)/shard_map/cst,td->csd/dot_general | solution.py:33
  24.8 0.1 broadcast_in_dim.6
  24.9 0.1 pad_maximum_fusion
  25.0 1.1 copy.31
  26.1 10.0 %all-to-all-done.1 = bf16[16,10,2048]{2,1,0:T(8,128)(2,1)} async-done(((bf16[16,10,2048]{2,1,0:T(8,128)(2,1)}), bf16[16,10,2048]{2,1,0:T(8,128)(2,1)}, u32[]{:S(2)}, u32[]{:S(2)}) %all-to-all-start.1) | async-done | bytes 655392 | tf_op jit(solution)/shard_map/all_to_all | solution.py:39
  36.2 5.8 %all-to-all-start = ((bf16[16,10,2176]{2,1,0:T(8,128)(2,1)}), bf16[16,10,2176]{2,1,0:T(8,128)(2,1)}, u32[]{:S(2)}, u32[]{:S(2)}) async-start(bf16[16,10,2176]{2,1,0:T(8,128)(2,1)} %copy.31), calls=%async_computation | async-start | bytes 2228224 | tf_op jit(solution)/shard_map/all_to_all | solution.py:40
  42.0 0.0 copy-done
  42.0 3.1 %fusion.2 = f32[16,10,768]{2,1,0:T(8,128)} fusion(bf16[16,10,2048]{2,1,0:T(8,128)(2,1)} %all-to-all-done.1, bf16[1,2048,768]{2,1,0:T(8,128)(2,1)S(1)} %copy-done), kind=kOutput, calls=%fused_computation.2 | convolution fusion | flops 503316480 | bytes 4292608 | tf_op jit(solution)/shard_map/gsd,df->gsf/dot_general | solution.py:43
  45.1 9.4 %all-to-all-done = bf16[16,10,2176]{2,1,0:T(8,128)(2,1)} async-done(((bf16[16,10,2176]{2,1,0:T(8,128)(2,1)}), bf16[16,10,2176]{2,1,0:T(8,128)(2,1)}, u32[]{:S(2)}, u32[]{:S(2)}) %all-to-all-start) | async-done | bytes 696352 | tf_op jit(solution)/shard_map/all_to_all | solution.py:40
  54.5 0.8 slice.16
  55.3 0.2 copy.48
  55.6 0.1 copy.33
  55.7 0.0 copy-start.2
  55.7 1.4 %slice.17 = bf16[16,10,2048]{2,1,0:T(8,128)(2,1)S(1)} slice(bf16[16,10,2176]{2,1,0:T(8,128)(2,1)} %all-to-all-done), slice={[0:16], [0:10], [0:2048]} | slice | bytes 1310720 | tf_op jit(solution)/shard_map/slice | solution.py:41
  57.1 0.0 copy-start.1
  57.1 1.0 copy-done.1
  58.1 0.0 copy-done.2
  58.1 3.2 %fusion.16 = f32[16,10]{0,1:T(8,128)S(1)} fusion(bf16[1,768,2048]{2,1,0:T(8,128)(2,1)} %param.11, bf16[16,10,2048]{2,1,0:T(8,128)(2,1)S(1)} %slice.17, f32[16,10,768]{2,1,0:T(8,128)S(1)} %copy-done.2), kind=kOutput, calls=%fused_computation.17 | convolution fusion | flops 504913760 | bytes 4293248 | tf_op jit(solution)/shard_map/gsf,fd->gsd/dot_general | solution.py:46
  61.2 5.8 %fusion.11 = bf16[16,10,2048]{2,0,1:T(8,128)(2,1)} fusion(bf16[1,2048,768]{2,1,0:T(8,128)(2,1)S(1)} %copy-done, bf16[1,768,2048]{2,1,0:T(8,128)(2,1)} %param.11, f32[16,10]{0,1:T(8,128)S(1)} %copy.33, bf16[16,10,2048]{2,1,0:T(8,128)(2,1)} %copy-done.1, f32[16,10,768]{2,1,0:T(8,128)} %fusion.2), kind=kOutput, calls=%fused_computation.10 | convolution fusion | flops 1009049600 | bytes 8094336 | tf_op jit(solution)/shard_map/gsf,df->gsd/dot_general | solution.py:54
  67.0 0.1 broadcast_in_dim.7
  67.1 1.1 pad_maximum_fusion.1
  68.3 1.2 copy.39
  69.5 5.7 %all-to-all-start.2 = ((bf16[16,10,2176]{2,1,0:T(8,128)(2,1)}), bf16[16,10,2176]{2,1,0:T(8,128)(2,1)}, u32[]{:S(2)}, u32[]{:S(2)}) async-start(bf16[16,10,2176]{2,1,0:T(8,128)(2,1)} %copy.39), calls=%async_computation.2 | async-start | bytes 2228224 | tf_op jit(solution)/shard_map/all_to_all | solution.py:58
  75.2 0.1 copy.42
  75.2 1.5 %multiply_reduce_fusion = f32[2048]{0:T(1024)S(1)} fusion(bf16[16,10,2048]{2,1,0:T(8,128)(2,1)} %all-to-all-done.1, f32[16,10]{1,0:T(8,128)S(1)} %copy.42), kind=kLoop, calls=%fused_computation.14 | loop fusion | flops 980992 | bytes 664192 | tf_op jit(solution)/shard_map/reduce_sum | solution.py:49
  76.8 2.5 %psum.21 = f32[2048]{0:T(1024)S(1)} all-reduce(f32[2048]{0:T(1024)S(1)} %multiply_reduce_fusion), channel_id=1, replica_groups=mesh['far'=8,'near'=4,'core'=2,'expert'=16] {'core'}, use_global_device_ids=true, to_apply=%region_5.6 | all-reduce | flops 2048 | bytes 16384 | tf_op jit(solution)/shard_map/psum | solution.py:10
  79.3 9.5 %psum.22 = f32[2048]{0:T(1024)S(1)} all-reduce(f32[2048]{0:T(1024)S(1)} %psum.21), channel_id=1, replica_groups=mesh['far'=8,'near'=4,'core'=2,'expert'=16] {'near'}, use_global_device_ids=true, to_apply=%region_6.7 | all-reduce | flops 2048 | bytes 16384 | tf_op jit(solution)/shard_map/psum | solution.py:10
  88.8 36.4 %psum.23 = f32[2048]{0:T(1024)S(1)} all-reduce(f32[2048]{0:T(1024)S(1)} %psum.22), channel_id=1, replica_groups=mesh['far'=8,'near'=4,'core'=2,'expert'=16] {'far'}, use_global_device_ids=true, to_apply=%region_7.8 | all-reduce | flops 2048 | bytes 16384 | tf_op jit(solution)/shard_map/psum | solution.py:10
  125.2 0.6 broadcast_multiply_fusion
  125.8 0.0 all-to-all-done.2
  125.8 1.3 slice.18
  127.1 1.3 %fusion.14 = bf16[128,2048]{1,0:T(8,128)(2,1)} fusion(bf16[16,10,2048]{2,1,0:T(8,128)(2,1)S(1)} %slice.18, f32[16,128]{1,0:T(8,128)S(1)} %fusion.52, pred[16,128]{1,0:T(8,128)(4,1)S(1)} %compare_bitcast_fusion), kind=kOutput, calls=%fused_computation.13 | convolution fusion | flops 84189184 | bytes 1189888 | tf_op jit(solution)/shard_map/cst,csd->td/dot_general | solution.py:63
  128.4 1.0 fusion.45
  129.5 0.6 select_reduce_fusion
  (5 shorter events, 0.1 us)
Async XLA Ops:
  0.6 41.3 %copy-start = (bf16[1,2048,768]{2,1,0:T(8,128)(2,1)S(1)}, bf16[1,2048,768]{2,1,0:T(8,128)(2,1)}, u32[]{:S(2)}) copy-start(bf16[1,2048,768]{2,1,0:T(8,128)(2,1)} %param.10) | copy-start | bytes 9437188
  6.0 30.2 %all-to-all-start.1 = ((bf16[16,10,2048]{2,1,0:T(8,128)(2,1)}), bf16[16,10,2048]{2,1,0:T(8,128)(2,1)}, u32[]{:S(2)}, u32[]{:S(2)}) async-start(bf16[16,10,2048]{2,1,0:T(8,128)(2,1)} %copy.35), calls=%async_computation.1 | async-start | bytes 2097152 | tf_op jit(solution)/shard_map/all_to_all | solution.py:39
  36.2 18.3 %all-to-all-start = ((bf16[16,10,2176]{2,1,0:T(8,128)(2,1)}), bf16[16,10,2176]{2,1,0:T(8,128)(2,1)}, u32[]{:S(2)}, u32[]{:S(2)}) async-start(bf16[16,10,2176]{2,1,0:T(8,128)(2,1)} %copy.31), calls=%async_computation | async-start | bytes 2228224 | tf_op jit(solution)/shard_map/all_to_all | solution.py:40
  55.7 2.4 %copy-start.2 = (f32[16,10,768]{2,1,0:T(8,128)S(1)}, f32[16,10,768]{2,1,0:T(8,128)}, u32[]{:S(2)}) copy-start(f32[16,10,768]{2,1,0:T(8,128)} %fusion.2) | copy-start | bytes 1474564
  57.1 1.0 copy-start.1
  69.5 56.3 %all-to-all-start.2 = ((bf16[16,10,2176]{2,1,0:T(8,128)(2,1)}), bf16[16,10,2176]{2,1,0:T(8,128)(2,1)}, u32[]{:S(2)}, u32[]{:S(2)}) async-start(bf16[16,10,2176]{2,1,0:T(8,128)(2,1)} %copy.39), calls=%async_computation.2 | async-start | bytes 2228224 | tf_op jit(solution)/shard_map/all_to_all | solution.py:58

commit v6 on v5

v6 whole, which is shorter than its diff:
```python
import jax
import jax.numpy as jnp
from jax import lax
from jax.sharding import Mesh, PartitionSpec as P

EXP_DEV = 8


def dp_sum(local_col):
    return lax.psum(lax.psum(lax.psum(local_col, "core"), "near"), "far")


def body(tokens, upstream, expert_ids, gate_weights, w_up, w_down):
    owners = lax.axis_size("expert")
    experts = EXP_DEV * owners
    tok_count, top = expert_ids.shape
    width = tokens.shape[1]
    column_tok = tok_count * lax.axis_size(("far", "near", "core"))
    most = tok_count * top // experts + tok_count * top // (4 * experts)
    slots = -(-most // 8) * 8
    rows_all = owners * slots
    up_mat = w_up[0]
    down_mat = w_down[0]
    live = expert_ids % EXP_DEV == 0
    target = expert_ids // EXP_DEV
    hit = (target[:, :, None] == jnp.arange(owners)[None, None, :]) & live[:, :, None]
    hit_f = hit.astype(jnp.float32)
    tok_oh = jnp.sum(hit_f, axis=1)
    lower = (jnp.arange(tok_count)[None, :] < jnp.arange(tok_count)[:, None]).astype(jnp.float32)
    before = jnp.dot(lower, tok_oh, preferred_element_type=jnp.float32)
    slot_hit = before.T[:, None, :] == jnp.arange(slots, dtype=jnp.float32)[None, :, None]
    pick3 = slot_hit & (tok_oh.T[:, None, :] > 0)
    pick = pick3.reshape(rows_all, tok_count).astype(jnp.bfloat16)
    gate_tc = jnp.sum(hit_f * gate_weights.astype(jnp.float32)[:, :, None], axis=1)
    send_x = jnp.dot(pick, tokens, preferred_element_type=jnp.float32)
    send_dy = jnp.dot(pick, upstream, preferred_element_type=jnp.float32)
    send_gate = jnp.einsum(
        "cst,tc->cs", pick3.astype(jnp.float32), gate_tc, preferred_element_type=jnp.float32
    ).reshape(rows_all)
    gate_cols = jnp.broadcast_to(send_gate[:, None], (rows_all, 128))
    packed = jnp.concatenate([send_x, send_dy, gate_cols], axis=1).astype(jnp.bfloat16)
    recv = lax.all_to_all(
        packed.reshape(owners, slots, -1), "expert", 0, 0, tiled=True
    ).reshape(rows_all, -1)
    rows_x = recv[:, :width]
    rows_dy = recv[:, width : 2 * width]
    rows_gate = recv[:, 2 * width]
    act = jnp.dot(rows_x, up_mat, preferred_element_type=jnp.float32)
    sig = jax.nn.sigmoid(act)
    hidden = (act * sig).astype(jnp.bfloat16)
    expert_out = jnp.dot(hidden, down_mat, preferred_element_type=jnp.float32)
    dy_wide = rows_dy.astype(jnp.float32)
    gate_term = jnp.sum(dy_wide * expert_out, axis=1)
    local_col = jnp.sum(gate_term[:, None] * rows_x.astype(jnp.float32), axis=0)
    router_grads = dp_sum(local_col) / jnp.float32(column_tok)
    scaled = (rows_gate.astype(jnp.float32)[:, None] * dy_wide).astype(jnp.bfloat16)
    back = lax.dot_general(
        scaled, down_mat, (((1,), (1,)), ((), ())), preferred_element_type=jnp.float32
    )
    act_grad = (back * sig * (1.0 + act * (1.0 - sig))).astype(jnp.bfloat16)
    route_grad = lax.dot_general(
        act_grad, up_mat, (((1,), (1,)), ((), ())), preferred_element_type=jnp.float32
    ).astype(jnp.bfloat16)
    gate_back = jnp.broadcast_to(gate_term.astype(jnp.bfloat16)[:, None], (rows_all, 128))
    returned = lax.all_to_all(
        jnp.concatenate([route_grad, gate_back], axis=1).reshape(owners, slots, -1),
        "expert",
        0,
        0,
        tiled=True,
    ).reshape(rows_all, -1)
    back_rows = returned[:, :width]
    back_gate = returned[:, width].astype(jnp.float32).reshape(owners, slots)
    token_grads = lax.dot_general(
        pick, back_rows, (((0,), (0,)), ((), ())), preferred_element_type=jnp.float32
    ).astype(jnp.bfloat16)
    gate_back_tc = jnp.einsum(
        "cst,cs->tc", pick3.astype(jnp.float32), back_gate, preferred_element_type=jnp.float32
    )
    gate_grads = jnp.sum(hit_f * gate_back_tc[:, None, :], axis=2).astype(jnp.bfloat16)
    return (token_grads, gate_grads, router_grads[None])


def solution(mesh):
    n_dp = mesh.shape["dp"]
    rows = ("far", "near", "core", "expert")
    split = Mesh(
        mesh.devices.reshape(n_dp // 8, 4, 2, mesh.shape["expert"]), rows
    )
    return jax.shard_map(
        body,
        mesh=split,
        in_specs=(
            P(rows, None),
            P(rows, None),
            P(rows, None),
            P(rows, None),
            P("expert", None, None),
            P("expert", None, None),
        ),
        out_specs=(P(rows, None), P(rows, None), P("expert", None)),
        check_vma=False,
    )
```

time: 131 us -> 119 us (0.908)
  the two profiles are of different devices: /device:TPU:2 before, /device:TPU:4 now
where the time goes in v6:
time: 119 us; the launch traced here: 118 us
  blocking collectives  86.4 us (73%)
  matrix products  13.4 us (11%)
  other arithmetic  7.81 us (7%)
  starting transfers between devices  6.3 us (5%)
  local copies, waits for them, and re-layouts  3.18 us (3%)
    psum x3, blocking collectives, dp_sum(): return lax.psum(lax.psum(lax.psum(local_col, 'core'), 'near'), 'far')  51.9 us
    all_to_all x1, blocking collectives, body(): lax.all_to_all(packed.reshape(owners, slots, -1), 'expert', 0, 0, tiled=T...  34.5 us
    all_to_all x1, starting transfers between devices, body(): lax.all_to_all(jnp.concatenate([route_grad, gate_back], axis=1).reshape(o...  6.3 us
    dot_general x1, matrix products, body(): lax.dot_general(act_grad, up_mat, (((1,), (1,)), ((), ())), preferred_ele...  5.59 us
    dot_general x1, matrix products, body(): lax.dot_general(pick, back_rows, (((0,), (0,)), ((), ())), preferred_elem...  2.38 us
  transfers between devices with their start and end apart: 1, of which 0 were waited for; matrix products, arithmetic and copies ran while one was open for 2% of the time, Pallas kernels for 0%

profile of v6, /device:TPU:4, one launch (start us, length us, event | category | flops | bytes accessed | tf_op | source)
XLA Modules:
  0.0 117.9 jit_solution(4629089403351243884)
XLA Ops:
  0.6 0.0 copy-start
  0.6 0.8 add_select_fusion.1
  1.5 0.8 fusion.58
  2.3 0.7 convert_element_type.47
  3.0 0.1 fusion.53
  3.1 0.2 fusion.43
  3.3 1.5 %convolution_convert_fusion = bf16[16,16,2048]{2,1,0:T(8,128)(2,1)S(1)} fusion(bf16[128,2048]{1,0:T(8,128)(2,1)} %param.7, f32[16,128]{1,0:T(8,128)S(1)} %fusion.53, pred[16,128]{1,0:T(8,128)(4,1)S(1)} %compare_bitcast_fusion), kind=kOutput, calls=%fused_computation.10 | convolution fusion | flops 134807552 | bytes 1583104 | tf_op jit(solution)/shard_map/dot_general | solution.py:36
  4.8 1.5 %convolution_convert_fusion.1 = bf16[16,16,2048]{2,1,0:T(8,128)(2,1)S(1)} fusion(bf16[128,2048]{1,0:T(8,128)(2,1)} %param.6, f32[16,128]{1,0:T(8,128)S(1)} %fusion.53, pred[16,128]{1,0:T(8,128)(4,1)S(1)} %compare_bitcast_fusion), kind=kOutput, calls=%fused_computation.11 | convolution fusion | flops 134807552 | bytes 1583104 | tf_op jit(solution)/shard_map/dot_general | solution.py:35
  6.3 0.1 broadcast_in_dim.6
  6.4 0.2 pad_maximum_fusion
  6.6 34.5 %all_to_all.10 = bf16[16,16,4224]{2,1,0:T(8,128)(2,1)S(1)} all-to-all(bf16[16,16,4224]{2,1,0:T(8,128)(2,1)S(1)} %pad_maximum_fusion), channel_id=1, replica_groups=mesh['far'=8,'near'=4,'core'=2,'expert'=16] {'expert'}, dimensions={0} | all-to-all | bytes 4325376 | tf_op jit(solution)/shard_map/all_to_all | solution.py:42
  41.1 0.0 copy-start.1
  41.1 0.1 convert_reduce_fusion
  41.2 0.0 copy-done
  41.2 0.0 copy-start.2
  41.2 1.0 fusion.2
  42.2 0.2 copy-done.1
  42.4 0.0 copy-start.3
  42.4 0.9 copy-done.3
  43.3 0.7 copy-done.2
  44.0 1.1 fusion.15
  45.1 5.6 %fusion.11 = bf16[256,2048]{1,0:T(8,128)(2,1)} fusion(bf16[1,2048,768]{2,1,0:T(8,128)(2,1)S(1)} %copy-done, bf16[1,768,2048]{2,1,0:T(8,128)(2,1)} %param.11, f32[256]{0:T(256)S(1)} %convert_reduce_fusion, bf16[256,4224]{1,0:T(8,128)(2,1)} %bitcast.58, f32[256,768]{1,0:T(8,128)} %copy-done.3), kind=kOutput, calls=%fused_computation.12 | convolution fusion | flops 1614479360 | bytes 9176064 | tf_op jit(solution)/shard_map/dot_general | solution.py:61
  50.7 0.1 broadcast_in_dim.7
  50.8 2.3 %pad_maximum_fusion.1 = bf16[256,2176]{1,0:T(8,128)(2,1)} fusion(bf16[256,128]{1,0:T(8,128)(2,1)S(1)} %broadcast_in_dim.7, bf16[256,2048]{1,0:T(8,128)(2,1)} %fusion.11), kind=kLoop, calls=%fused_computation.21 | loop fusion | flops 2228224 | bytes 2228224 | tf_op jit(solution)/shard_map/concatenate | solution.py:66
  53.1 6.3 %all-to-all-start.1 = ((bf16[16,16,2176]{2,1,0:T(8,128)(2,1)}), bf16[16,16,2176]{2,1,0:T(8,128)(2,1)}, u32[]{:S(2)}, u32[]{:S(2)}) async-start(bf16[16,16,2176]{2,1,0:T(8,128)(2,1)} %bitcast.60), calls=%async_computation.1 | async-start | bytes 2228224 | tf_op jit(solution)/shard_map/all_to_all | solution.py:65
  59.5 0.1 eq.52
  59.5 0.1 fusion.47
  59.7 1.5 %multiply_reduce_fusion = f32[2048]{0:T(1024)S(1)} fusion(f32[256]{0:T(256)S(1)} %fusion.15, bf16[256,4224]{1,0:T(8,128)(2,1)} %bitcast.59), kind=kLoop, calls=%fused_computation.16 | loop fusion | flops 1570816 | bytes 1057792 | tf_op jit(solution)/shard_map/reduce_sum | solution.py:54
  61.2 2.5 %psum.21 = f32[2048]{0:T(1024)S(1)} all-reduce(f32[2048]{0:T(1024)S(1)} %multiply_reduce_fusion), channel_id=1, replica_groups=mesh['far'=8,'near'=4,'core'=2,'expert'=16] {'core'}, use_global_device_ids=true, to_apply=%region_5.6 | all-reduce | flops 2048 | bytes 16384 | tf_op jit(solution)/shard_map/psum | solution.py:10
  63.7 12.9 %psum.22 = f32[2048]{0:T(1024)S(1)} all-reduce(f32[2048]{0:T(1024)S(1)} %psum.21), channel_id=1, replica_groups=mesh['far'=8,'near'=4,'core'=2,'expert'=16] {'near'}, use_global_device_ids=true, to_apply=%region_6.7 | all-reduce | flops 2048 | bytes 16384 | tf_op jit(solution)/shard_map/psum | solution.py:10
  76.6 36.5 %psum.23 = f32[2048]{0:T(1024)S(1)} all-reduce(f32[2048]{0:T(1024)S(1)} %psum.22), channel_id=1, replica_groups=mesh['far'=8,'near'=4,'core'=2,'expert'=16] {'far'}, use_global_device_ids=true, to_apply=%region_7.8 | all-reduce | flops 2048 | bytes 16384 | tf_op jit(solution)/shard_map/psum | solution.py:10
  113.1 0.6 broadcast_multiply_fusion
  113.7 0.0 all-to-all-done.1
  113.7 0.9 slice_reduce_fusion
  114.6 2.4 %convolution_convert_fusion.2 = bf16[128,2048]{1,0:T(8,128)(2,1)} fusion(pred[256,128]{1,0:T(32,128)(4,1)S(1)} %fusion.47, bf16[256,2176]{1,0:T(8,128)(2,1)} %bitcast.13), kind=kOutput, calls=%fused_computation.13 | convolution fusion | flops 134479872 | bytes 1605632 | tf_op jit(solution)/shard_map/dot_general | solution.py:74
  117.0 0.1 reshape.66
  117.1 0.2 fusion.41
  117.3 0.6 select_reduce_fusion
  (5 shorter events, 0.0 us)
Async XLA Ops:
  0.6 40.5 %copy-start = (bf16[1,2048,768]{2,1,0:T(8,128)(2,1)S(1)}, bf16[1,2048,768]{2,1,0:T(8,128)(2,1)}, u32[]{:S(2)}) copy-start(bf16[1,2048,768]{2,1,0:T(8,128)(2,1)} %param.10) | copy-start | bytes 9437188
  41.1 1.4 %copy-start.1 = (bf16[16,16,4224]{2,1,0:T(8,128)(2,1)}, bf16[16,16,4224]{2,1,0:T(8,128)(2,1)S(1)}, u32[]{:S(2)}) copy-start(bf16[16,16,4224]{2,1,0:T(8,128)(2,1)S(1)} %all_to_all.10) | copy-start | bytes 6488068
  41.2 2.8 %copy-start.2 = (bf16[1,768,2048]{2,1,0:T(8,128)(2,1)S(1)}, bf16[1,768,2048]{2,1,0:T(8,128)(2,1)}, u32[]{:S(2)}) copy-start(bf16[1,768,2048]{2,1,0:T(8,128)(2,1)} %param.11) | copy-start | bytes 9437188
  42.4 0.9 copy-start.3
  53.1 60.5 %all-to-all-start.1 = ((bf16[16,16,2176]{2,1,0:T(8,128)(2,1)}), bf16[16,16,2176]{2,1,0:T(8,128)(2,1)}, u32[]{:S(2)}, u32[]{:S(2)}) async-start(bf16[16,16,2176]{2,1,0:T(8,128)(2,1)} %bitcast.60), calls=%async_computation.1 | async-start | bytes 2228224 | tf_op jit(solution)/shard_map/all_to_all | solution.py:65

commit v7 on v6

--- a/solution.py
+++ b/solution.py
@@ -17,7 +17,7 @@
     width = tokens.shape[1]
     column_tok = tok_count * lax.axis_size(("far", "near", "core"))
     most = tok_count * top // experts + tok_count * top // (4 * experts)
-    slots = -(-most // 8) * 8
+    slots = -(-(most + 1) // 8) * 8
     rows_all = owners * slots
     up_mat = w_up[0]
     down_mat = w_down[0]
@@ -37,14 +37,16 @@
     send_gate = jnp.einsum(
         "cst,tc->cs", pick3.astype(jnp.float32), gate_tc, preferred_element_type=jnp.float32
     ).reshape(rows_all)
-    gate_cols = jnp.broadcast_to(send_gate[:, None], (rows_all, 128))
-    packed = jnp.concatenate([send_x, send_dy, gate_cols], axis=1).astype(jnp.bfloat16)
+    gate_rows = jnp.pad(
+        send_gate.reshape(owners, 1, slots), ((0, 0), (slots - 1, 0), (0, width - slots))
+    ).reshape(rows_all, width)
+    packed = jnp.concatenate([send_x, send_dy + gate_rows], axis=1).astype(jnp.bfloat16)
     recv = lax.all_to_all(
         packed.reshape(owners, slots, -1), "expert", 0, 0, tiled=True
     ).reshape(rows_all, -1)
     rows_x = recv[:, :width]
     rows_dy = recv[:, width : 2 * width]
-    rows_gate = recv[:, 2 * width]
+    rows_gate = recv.reshape(owners, slots, -1)[:, slots - 1, width : width + slots].reshape(rows_all)
     act = jnp.dot(rows_x, up_mat, preferred_element_type=jnp.float32)
     sig = jax.nn.sigmoid(act)
     hidden = (act * sig).astype(jnp.bfloat16)
@@ -61,16 +63,19 @@
     route_grad = lax.dot_general(
         act_grad, up_mat, (((1,), (1,)), ((), ())), preferred_element_type=jnp.float32
     ).astype(jnp.bfloat16)
-    gate_back = jnp.broadcast_to(gate_term.astype(jnp.bfloat16)[:, None], (rows_all, 128))
+    gate_back = jnp.pad(
+        gate_term.astype(jnp.bfloat16).reshape(owners, 1, slots),
+        ((0, 0), (slots - 1, 0), (0, width - slots)),
+    ).reshape(rows_all, width)
     returned = lax.all_to_all(
-        jnp.concatenate([route_grad, gate_back], axis=1).reshape(owners, slots, -1),
+        (route_grad + gate_back).reshape(owners, slots, -1),
         "expert",
         0,
         0,
         tiled=True,
     ).reshape(rows_all, -1)
-    back_rows = returned[:, :width]
-    back_gate = returned[:, width].astype(jnp.float32).reshape(owners, slots)
+    back_rows = returned
+    back_gate = returned.reshape(owners, slots, -1)[:, slots - 1, :slots].astype(jnp.float32)
     token_grads = lax.dot_general(
         pick, back_rows, (((0,), (0,)), ((), ())), preferred_element_type=jnp.float32
     ).astype(jnp.bfloat16)

time: 119 us -> 116 us (0.975)
  the two profiles are of different devices: /device:TPU:4 before, /device:TPU:2 now
where the time goes in v7:
time: 116 us
  blocking collectives  86.4 us (74%)
  matrix products  13.5 us (12%)
  other arithmetic  6.22 us (5%)
  starting transfers between devices  5.48 us (5%)
  local copies, waits for them, and re-layouts  3.27 us (3%)
    psum x3, blocking collectives, dp_sum(): return lax.psum(lax.psum(lax.psum(local_col, 'core'), 'near'), 'far')  51.8 us
    all_to_all x1, blocking collectives, body(): lax.all_to_all(packed.reshape(owners, slots, -1), 'expert', 0, 0, tiled=T...  34.6 us
    dot_general x1, matrix products, body(): lax.dot_general(act_grad, up_mat, (((1,), (1,)), ((), ())), preferred_ele...  5.9 us
    all_to_all x1, starting transfers between devices, body(): lax.all_to_all((route_grad + gate_back).reshape(owners, slots, -1), 'expe...  5.48 us
    dot_general x1, matrix products, body(): lax.dot_general(pick, back_rows, (((0,), (0,)), ((), ())), preferred_elem...  2.38 us
  transfers between devices with their start and end apart: 1, of which 0 were waited for; matrix products, arithmetic and copies ran while one was open for 2% of the time, Pallas kernels for 0%

profile of v7, /device:TPU:2, one launch (start us, length us, event | category | flops | bytes accessed | tf_op | source)
XLA Modules:
  0.0 115.6 jit_solution(9974678353978137599)
XLA Ops:
  0.6 0.0 copy-start
  0.6 0.8 add_select_fusion.1
  1.5 0.8 fusion.62
  2.3 0.7 convert_element_type.65
  3.0 0.1 fusion.56
  3.2 0.1 eq.53
  3.3 0.0 copy-start.2
  3.3 0.1 fusion.47
  3.4 0.1 fusion.50
  3.5 1.5 %convolution_convert_fusion = bf16[16,16,2048]{2,1,0:T(8,128)(2,1)S(1)} fusion(bf16[128,2048]{1,0:T(8,128)(2,1)} %param.6, f32[16,128]{1,0:T(8,128)S(1)} %fusion.56, pred[16,128]{1,0:T(8,128)(4,1)S(1)} %compare_bitcast_fusion), kind=kOutput, calls=%fused_computation.11 | convolution fusion | flops 134807552 | bytes 1583104 | tf_op jit(solution)/shard_map/dot_general | solution.py:35
  5.0 0.2 pad.8
  5.2 0.0 copy-done.2
  5.3 0.4 fusion.11
  5.7 0.2 pad_maximum_fusion
  5.9 34.6 %all_to_all.10 = bf16[16,16,4096]{2,1,0:T(8,128)(2,1)S(1)} all-to-all(bf16[16,16,4096]{2,1,0:T(8,128)(2,1)S(1)} %pad_maximum_fusion), channel_id=1, replica_groups=mesh['far'=8,'near'=4,'core'=2,'expert'=16] {'expert'}, dimensions={0} | all-to-all | bytes 4194304 | tf_op jit(solution)/shard_map/all_to_all | solution.py:44
  40.5 0.0 copy-start.1
  40.5 0.0 copy-done
  40.5 0.0 copy-start.3
  40.5 1.0 fusion.2
  41.5 0.4 copy-done.1
  41.8 1.3 %copy-done.3 = bf16[1,768,2048]{2,1,0:T(8,128)(2,1)S(1)} copy-done((bf16[1,768,2048]{2,1,0:T(8,128)(2,1)S(1)}, bf16[1,768,2048]{2,1,0:T(8,128)(2,1)}, u32[]{:S(2)}) %copy-start.3) | copy-done | bytes 3145752
  43.1 0.0 copy-start.4
  43.1 1.1 fusion.20
  44.2 0.0 copy-done.4
  44.3 0.1 convert_element_type.79
  44.4 0.8 fusion.61
  45.1 0.1 reshape.64
  45.2 1.1 pad.9.clone
  46.3 5.9 %fusion.15 = bf16[256,2048]{1,0:T(8,128)(2,1)} fusion(bf16[256,2048]{1,0:T(8,128)(2,1)} %bitcast.71, bf16[1,2048,768]{2,1,0:T(8,128)(2,1)S(1)} %copy-done, bf16[1,768,2048]{2,1,0:T(8,128)(2,1)} %param.11, f32[256]{0:T(256)S(1)} %reshape.64, bf16[256,4096]{1,0:T(8,128)(2,1)} %bitcast.67, f32[256,768]{1,0:T(8,128)} %copy-done.4), kind=kOutput, calls=%fused_computation.15 | convolution fusion | flops 1616576512 | bytes 10224640 | tf_op jit(solution)/shard_map/dot_general | solution.py:63
  52.2 5.5 %all-to-all-start.1 = ((bf16[16,16,2048]{2,1,0:T(8,128)(2,1)}), bf16[16,16,2048]{2,1,0:T(8,128)(2,1)}, u32[]{:S(2)}, u32[]{:S(2)}) async-start(bf16[16,16,2048]{2,1,0:T(8,128)(2,1)} %bitcast.70), calls=%async_computation.1 | async-start | bytes 2097152 | tf_op jit(solution)/shard_map/all_to_all | solution.py:70
  57.7 1.5 %multiply_reduce_fusion = f32[2048]{0:T(1024)S(1)} fusion(f32[256]{0:T(256)S(1)} %fusion.20, bf16[256,4096]{1,0:T(8,128)(2,1)} %bitcast.68), kind=kLoop, calls=%fused_computation.19 | loop fusion | flops 1570816 | bytes 1057792 | tf_op jit(solution)/shard_map/reduce_sum | solution.py:56
  59.2 2.5 %psum.21 = f32[2048]{0:T(1024)S(1)} all-reduce(f32[2048]{0:T(1024)S(1)} %multiply_reduce_fusion), channel_id=1, replica_groups=mesh['far'=8,'near'=4,'core'=2,'expert'=16] {'core'}, use_global_device_ids=true, to_apply=%region_5.6 | all-reduce | flops 2048 | bytes 16384 | tf_op jit(solution)/shard_map/psum | solution.py:10
  61.7 12.9 %psum.22 = f32[2048]{0:T(1024)S(1)} all-reduce(f32[2048]{0:T(1024)S(1)} %psum.21), channel_id=1, replica_groups=mesh['far'=8,'near'=4,'core'=2,'expert'=16] {'near'}, use_global_device_ids=true, to_apply=%region_6.7 | all-reduce | flops 2048 | bytes 16384 | tf_op jit(solution)/shard_map/psum | solution.py:10
  74.7 36.4 %psum.23 = f32[2048]{0:T(1024)S(1)} all-reduce(f32[2048]{0:T(1024)S(1)} %psum.22), channel_id=1, replica_groups=mesh['far'=8,'near'=4,'core'=2,'expert'=16] {'far'}, use_global_device_ids=true, to_apply=%region_7.8 | all-reduce | flops 2048 | bytes 16384 | tf_op jit(solution)/shard_map/psum | solution.py:10
  111.1 0.6 broadcast_multiply_fusion
  111.7 0.0 all-to-all-done.1
  111.7 0.9 fusion.44
  112.6 0.6 select_reduce_fusion
  113.2 2.4 %fusion.18 = bf16[128,2048]{1,0:T(8,128)(2,1)} fusion(bf16[16,16,2048]{2,1,0:T(8,128)(2,1)} %all-to-all-done.1, f32[16,128]{1,0:T(8,128)S(1)} %fusion.56, pred[16,128]{1,0:T(8,128)(4,1)S(1)} %compare_bitcast_fusion), kind=kOutput, calls=%fused_computation.16 | convolution fusion | flops 134545408 | bytes 1583104 | tf_op jit(solution)/shard_map/dot_general | solution.py:79
  (4 shorter events, 0.1 us)
Async XLA Ops:
  0.6 39.8 %copy-start = (bf16[1,2048,768]{2,1,0:T(8,128)(2,1)S(1)}, bf16[1,2048,768]{2,1,0:T(8,128)(2,1)}, u32[]{:S(2)}) copy-start(bf16[1,2048,768]{2,1,0:T(8,128)(2,1)} %param.10) | copy-start | bytes 9437188
  3.3 2.0 %copy-start.2 = (bf16[128,2048]{1,0:T(8,128)(2,1)S(1)}, bf16[128,2048]{1,0:T(8,128)(2,1)}, u32[]{:S(2)}) copy-start(bf16[128,2048]{1,0:T(8,128)(2,1)} %param.7) | copy-start | bytes 1572868
  40.5 1.4 %copy-start.1 = (bf16[16,16,4096]{2,1,0:T(8,128)(2,1)}, bf16[16,16,4096]{2,1,0:T(8,128)(2,1)S(1)}, u32[]{:S(2)}) copy-start(bf16[16,16,4096]{2,1,0:T(8,128)(2,1)S(1)} %all_to_all.10) | copy-start | bytes 6291460
  40.5 2.6 %copy-start.3 = (bf16[1,768,2048]{2,1,0:T(8,128)(2,1)S(1)}, bf16[1,768,2048]{2,1,0:T(8,128)(2,1)}, u32[]{:S(2)}) copy-start(bf16[1,768,2048]{2,1,0:T(8,128)(2,1)} %param.11) | copy-start | bytes 9437188
  43.1 1.1 copy-start.4
  52.2 59.4 %all-to-all-start.1 = ((bf16[16,16,2048]{2,1,0:T(8,128)(2,1)}), bf16[16,16,2048]{2,1,0:T(8,128)(2,1)}, u32[]{:S(2)}, u32[]{:S(2)}) async-start(bf16[16,16,2048]{2,1,0:T(8,128)(2,1)} %bitcast.70), calls=%async_computation.1 | async-start | bytes 2097152 | tf_op jit(solution)/shard_map/all_to_all | solution.py:70

commit v8 on v7

--- a/solution.py
+++ b/solution.py
@@ -8,6 +8,13 @@
 
 def dp_sum(local_col):
     return lax.psum(lax.psum(lax.psum(local_col, "core"), "near"), "far")
+
+
+def dense_all_to_all(blocks, used):
+    owners, slots, cols = blocks.shape
+    flat = blocks[:, :used, :].reshape(owners, 8, used * cols // 8)
+    moved = lax.all_to_all(flat, "expert", 0, 0, tiled=True).reshape(owners, used, cols)
+    return jnp.pad(moved, ((0, 0), (0, slots - used), (0, 0)))
 
 
 def body(tokens, upstream, expert_ids, gate_weights, w_up, w_down):
@@ -38,15 +45,14 @@
         "cst,tc->cs", pick3.astype(jnp.float32), gate_tc, preferred_element_type=jnp.float32
     ).reshape(rows_all)
     gate_rows = jnp.pad(
-        send_gate.reshape(owners, 1, slots), ((0, 0), (slots - 1, 0), (0, width - slots))
+        send_gate.reshape(owners, 1, slots),
+        ((0, 0), (most, slots - 1 - most), (0, width - slots)),
     ).reshape(rows_all, width)
     packed = jnp.concatenate([send_x, send_dy + gate_rows], axis=1).astype(jnp.bfloat16)
-    recv = lax.all_to_all(
-        packed.reshape(owners, slots, -1), "expert", 0, 0, tiled=True
-    ).reshape(rows_all, -1)
+    recv = dense_all_to_all(packed.reshape(owners, slots, -1), most + 1).reshape(rows_all, -1)
     rows_x = recv[:, :width]
     rows_dy = recv[:, width : 2 * width]
-    rows_gate = recv.reshape(owners, slots, -1)[:, slots - 1, width : width + slots].reshape(rows_all)
+    rows_gate = recv.reshape(owners, slots, -1)[:, most, width : width + slots].reshape(rows_all)
     act = jnp.dot(rows_x, up_mat, preferred_element_type=jnp.float32)
     sig = jax.nn.sigmoid(act)
     hidden = (act * sig).astype(jnp.bfloat16)

time: 116 us -> 121 us (1.043)
  local copies, waits for them, and re-layouts: 3.27 us -> 13.6 us
  blocking collectives: 86.4 us -> 79.6 us
  other arithmetic: 6.22 us -> 7.57 us
    reshape x0 -> x2, local copies, waits for them, and re-layouts: none -> 8.52 us  [the longest x1 4.27 us: dense_all_to_all(): flat = blocks[:, :used, :].reshape(owners, 8, used * cols // 8)]
    psum x3, blocking collectives: 51.8 us -> 48.4 us  [dp_sum(): return lax.psum(lax.psum(lax.psum(local_col, 'core'), 'near'), 'far')]
    all_to_all x1, blocking collectives: 34.6 us -> 31.2 us  [dense_all_to_all(): lax.all_to_all(flat, 'expert', 0, 0, tiled=True).reshape(owners, used, cols)]
    pad x1 -> x2, local copies, waits for them, and re-layouts: 0.23 us -> 2.09 us  [the longest x1 1.86 us: dense_all_to_all(): return jnp.pad(moved, ((0, 0), (0, slots - used), (0, 0)))]
    concatenate x1, other arithmetic: 0.21 us -> 1.57 us  [body(): jnp.concatenate([send_x, send_dy + gate_rows], axis=1).astype(jnp.bfloat16)]
where the time goes in v8:
time: 121 us
  blocking collectives  79.6 us (66%)
  local copies, waits for them, and re-layouts  13.6 us (11%)
  matrix products  13.5 us (11%)
  other arithmetic  7.57 us (6%)
  starting transfers between devices  5.52 us (5%)
    psum x3, blocking collectives, dp_sum(): return lax.psum(lax.psum(lax.psum(local_col, 'core'), 'near'), 'far')  48.4 us
    all_to_all x1, blocking collectives, dense_all_to_all(): lax.all_to_all(flat, 'expert', 0, 0, tiled=True).reshape(owners, used, cols)  31.2 us
    dot_general x1, matrix products, body(): lax.dot_general(act_grad, up_mat, (((1,), (1,)), ((), ())), preferred_ele...  5.9 us
    all_to_all x1, starting transfers between devices, body(): lax.all_to_all((route_grad + gate_back).reshape(owners, slots, -1), 'expe...  5.52 us
    reshape x1, local copies, waits for them, and re-layouts, dense_all_to_all(): flat = blocks[:, :used, :].reshape(owners, 8, used * cols // 8)  4.27 us
    reshape x1, local copies, waits for them, and re-layouts, dense_all_to_all(): lax.all_to_all(flat, 'expert', 0, 0, tiled=True).reshape(owners, used, cols)  4.26 us
  transfers between devices with their start and end apart: 1, of which 0 were waited for; matrix products, arithmetic and copies ran while one was open for 2% of the time, Pallas kernels for 0%

profile of v8, /device:TPU:2, one launch (start us, length us, event | category | flops | bytes accessed | tf_op | source)
XLA Modules:
  0.0 120.7 jit_solution(15372305774584903273)
XLA Ops:
  0.6 0.0 copy-start
  0.6 0.9 fusion.62
  1.5 0.8 add_select_fusion.1
  2.3 0.7 convert_element_type.67
  3.0 0.1 fusion.56
  3.2 0.1 eq.53
  3.3 0.0 copy-start.2
  3.3 0.2 fusion.47
  3.4 0.1 fusion.50
  3.5 1.5 %convolution_convert_fusion = bf16[16,16,2048]{2,1,0:T(8,128)(2,1)S(1)} fusion(bf16[128,2048]{1,0:T(8,128)(2,1)} %param.6, f32[16,128]{1,0:T(8,128)S(1)} %fusion.56, pred[16,128]{1,0:T(8,128)(4,1)S(1)} %compare_bitcast_fusion), kind=kOutput, calls=%fused_computation.11 | convolution fusion | flops 134807552 | bytes 1583104 | tf_op jit(solution)/shard_map/dot_general | solution.py:42
  5.0 0.2 pad.12
  5.2 0.0 copy-done.2
  5.3 0.4 fusion.11
  5.7 1.6 %pad_maximum_fusion = bf16[16,11,4096]{2,1,0:T(8,128)(2,1)} fusion(bf16[16,16,2048]{2,1,0:T(8,128)(2,1)S(1)} %bitcast.69, bf16[16,16,2048]{2,1,0:T(8,128)(2,1)S(1)} %convolution_convert_fusion), kind=kLoop, calls=%fused_computation.18 | loop fusion | flops 2883584 | bytes 3538944 | tf_op jit(solution)/shard_map/concatenate | solution.py:51
  7.3 4.3 %reshape.67 = bf16[16,8,5632]{2,1,0:T(8,128)(2,1)} reshape(bf16[16,11,4096]{2,1,0:T(8,128)(2,1)} %pad_maximum_fusion) | data formatting | bytes 2883584 | tf_op jit(solution)/shard_map/reshape | solution.py:15
  11.5 31.2 %all_to_all.10 = bf16[16,8,5632]{2,1,0:T(8,128)(2,1)} all-to-all(bf16[16,8,5632]{2,1,0:T(8,128)(2,1)} %reshape.67), channel_id=1, replica_groups=mesh['far'=8,'near'=4,'core'=2,'expert'=16] {'expert'}, dimensions={0} | all-to-all | bytes 2883584 | tf_op jit(solution)/shard_map/all_to_all | solution.py:16
  42.8 4.3 %reshape.68 = bf16[16,11,4096]{2,1,0:T(8,128)(2,1)} reshape(bf16[16,8,5632]{2,1,0:T(8,128)(2,1)} %all_to_all.10) | data formatting | bytes 2883584 | tf_op jit(solution)/shard_map/reshape | solution.py:16
  47.0 0.8 fusion.61
  47.8 0.1 reshape.72
  47.9 1.9 %pad.13 = bf16[16,16,4096]{2,1,0:T(8,128)(2,1)S(1)} pad(bf16[16,11,4096]{2,1,0:T(8,128)(2,1)} %reshape.68, bf16[]{:T(256)} %constant.40.clone.1), padding=0_0x0_5x0_0 | pad | bytes 3538946 | tf_op jit(solution)/shard_map/jit(_pad)/pad | solution.py:17
  49.8 0.0 copy-start.1
  49.8 0.0 copy-done
  49.8 0.0 copy-start.3
  49.8 1.0 fusion.2
  50.8 0.3 copy-done.1
  51.1 1.3 %copy-done.3 = bf16[1,768,2048]{2,1,0:T(8,128)(2,1)S(1)} copy-done((bf16[1,768,2048]{2,1,0:T(8,128)(2,1)S(1)}, bf16[1,768,2048]{2,1,0:T(8,128)(2,1)}, u32[]{:S(2)}) %copy-start.3) | copy-done | bytes 3145752
  52.4 0.0 copy-start.4
  52.4 1.2 fusion.20
  53.6 0.0 copy-done.4
  53.6 0.1 convert_element_type.81
  53.7 1.1 pad.14.clone
  54.8 5.9 %fusion.15 = bf16[256,2048]{1,0:T(8,128)(2,1)} fusion(bf16[256,2048]{1,0:T(8,128)(2,1)} %bitcast.71, bf16[1,2048,768]{2,1,0:T(8,128)(2,1)S(1)} %copy-done, bf16[1,768,2048]{2,1,0:T(8,128)(2,1)} %param.11, f32[256]{0:T(256)S(1)} %reshape.72, bf16[256,4096]{1,0:T(8,128)(2,1)} %bitcast.67, f32[256,768]{1,0:T(8,128)} %copy-done.4), kind=kOutput, calls=%fused_computation.15 | convolution fusion | flops 1616576512 | bytes 10224640 | tf_op jit(solution)/shard_map/dot_general | solution.py:69
  60.7 5.5 %all-to-all-start.1 = ((bf16[16,16,2048]{2,1,0:T(8,128)(2,1)}), bf16[16,16,2048]{2,1,0:T(8,128)(2,1)}, u32[]{:S(2)}, u32[]{:S(2)}) async-start(bf16[16,16,2048]{2,1,0:T(8,128)(2,1)} %bitcast.70), calls=%async_computation.1 | async-start | bytes 2097152 | tf_op jit(solution)/shard_map/all_to_all | solution.py:76
  66.2 1.5 %multiply_reduce_fusion = f32[2048]{0:T(1024)S(1)} fusion(f32[256]{0:T(256)S(1)} %fusion.20, bf16[256,4096]{1,0:T(8,128)(2,1)} %bitcast.68), kind=kLoop, calls=%fused_computation.19 | loop fusion | flops 1570816 | bytes 1057792 | tf_op jit(solution)/shard_map/reduce_sum | solution.py:62
  67.8 2.5 %psum.21 = f32[2048]{0:T(1024)S(1)} all-reduce(f32[2048]{0:T(1024)S(1)} %multiply_reduce_fusion), channel_id=1, replica_groups=mesh['far'=8,'near'=4,'core'=2,'expert'=16] {'core'}, use_global_device_ids=true, to_apply=%region_5.6 | all-reduce | flops 2048 | bytes 16384 | tf_op jit(solution)/shard_map/psum | solution.py:10
  70.3 9.5 %psum.22 = f32[2048]{0:T(1024)S(1)} all-reduce(f32[2048]{0:T(1024)S(1)} %psum.21), channel_id=1, replica_groups=mesh['far'=8,'near'=4,'core'=2,'expert'=16] {'near'}, use_global_device_ids=true, to_apply=%region_6.7 | all-reduce | flops 2048 | bytes 16384 | tf_op jit(solution)/shard_map/psum | solution.py:10
  79.7 36.4 %psum.23 = f32[2048]{0:T(1024)S(1)} all-reduce(f32[2048]{0:T(1024)S(1)} %psum.22), channel_id=1, replica_groups=mesh['far'=8,'near'=4,'core'=2,'expert'=16] {'far'}, use_global_device_ids=true, to_apply=%region_7.8 | all-reduce | flops 2048 | bytes 16384 | tf_op jit(solution)/shard_map/psum | solution.py:10
  116.2 0.6 broadcast_multiply_fusion
  116.8 0.0 all-to-all-done.1
  116.8 0.9 fusion.44
  117.7 0.6 select_reduce_fusion
  118.3 2.4 %fusion.18 = bf16[128,2048]{1,0:T(8,128)(2,1)} fusion(bf16[16,16,2048]{2,1,0:T(8,128)(2,1)} %all-to-all-done.1, f32[16,128]{1,0:T(8,128)S(1)} %fusion.56, pred[16,128]{1,0:T(8,128)(4,1)S(1)} %compare_bitcast_fusion), kind=kOutput, calls=%fused_computation.16 | convolution fusion | flops 134545408 | bytes 1583104 | tf_op jit(solution)/shard_map/dot_general | solution.py:85
  (4 shorter events, 0.0 us)
Async XLA Ops:
  0.6 49.1 %copy-start = (bf16[1,2048,768]{2,1,0:T(8,128)(2,1)S(1)}, bf16[1,2048,768]{2,1,0:T(8,128)(2,1)}, u32[]{:S(2)}) copy-start(bf16[1,2048,768]{2,1,0:T(8,128)(2,1)} %param.10) | copy-start | bytes 9437188
  3.3 2.0 %copy-start.2 = (bf16[128,2048]{1,0:T(8,128)(2,1)S(1)}, bf16[128,2048]{1,0:T(8,128)(2,1)}, u32[]{:S(2)}) copy-start(bf16[128,2048]{1,0:T(8,128)(2,1)} %param.7) | copy-start | bytes 1572868
  49.8 1.4 %copy-start.1 = (bf16[16,16,4096]{2,1,0:T(8,128)(2,1)}, bf16[16,16,4096]{2,1,0:T(8,128)(2,1)S(1)}, u32[]{:S(2)}) copy-start(bf16[16,16,4096]{2,1,0:T(8,128)(2,1)S(1)} %pad.13) | copy-start | bytes 6291460
  49.8 2.6 %copy-start.3 = (bf16[1,768,2048]{2,1,0:T(8,128)(2,1)S(1)}, bf16[1,768,2048]{2,1,0:T(8,128)(2,1)}, u32[]{:S(2)}) copy-start(bf16[1,768,2048]{2,1,0:T(8,128)(2,1)} %param.11) | copy-start | bytes 9437188
  52.4 1.2 copy-start.4
  60.7 56.0 %all-to-all-start.1 = ((bf16[16,16,2048]{2,1,0:T(8,128)(2,1)}), bf16[16,16,2048]{2,1,0:T(8,128)(2,1)}, u32[]{:S(2)}, u32[]{:S(2)}) async-start(bf16[16,16,2048]{2,1,0:T(8,128)(2,1)} %bitcast.70), calls=%async_computation.1 | async-start | bytes 2097152 | tf_op jit(solution)/shard_map/all_to_all | solution.py:76

commit v9 on v7

--- a/solution.py
+++ b/solution.py
@@ -7,7 +7,7 @@
 
 
 def dp_sum(local_col):
-    return lax.psum(lax.psum(lax.psum(local_col, "core"), "near"), "far")
+    return lax.psum(lax.psum(lax.psum(local_col, "far"), "near"), "core")
 
 
 def body(tokens, upstream, expert_ids, gate_weights, w_up, w_down):

time: 116 us -> 117 us (level)
  the two profiles are of different devices: /device:TPU:2 before, /device:TPU:1 now
where the time goes in v9:
time: 117 us; the launch traced here: 116 us
  blocking collectives  88.4 us (76%)
  matrix products  13.5 us (12%)
  other arithmetic  6.22 us (5%)
  starting transfers between devices  4.34 us (4%)
  local copies, waits for them, and re-layouts  3.27 us (3%)
    psum x3, blocking collectives, dp_sum(): return lax.psum(lax.psum(lax.psum(local_col, 'far'), 'near'), 'core')  61.9 us
    all_to_all x1, blocking collectives, body(): lax.all_to_all(packed.reshape(owners, slots, -1), 'expert', 0, 0, tiled=T...  26.5 us
    dot_general x1, matrix products, body(): lax.dot_general(act_grad, up_mat, (((1,), (1,)), ((), ())), preferred_ele...  5.9 us
    all_to_all x1, starting transfers between devices, body(): lax.all_to_all((route_grad + gate_back).reshape(owners, slots, -1), 'expe...  4.34 us
    dot_general x1, matrix products, body(): lax.dot_general(pick, back_rows, (((0,), (0,)), ((), ())), preferred_elem...  2.38 us
  transfers between devices with their start and end apart: 1, of which 0 were waited for; matrix products, arithmetic and copies ran while one was open for 2% of the time, Pallas kernels for 0%

profile of v9, /device:TPU:1, one launch (start us, length us, event | category | flops | bytes accessed | tf_op | source)
XLA Modules:
  0.0 116.4 jit_solution(13853494643631511233)
XLA Ops:
  0.6 0.0 copy-start
  0.6 0.8 add_select_fusion.1
  1.5 0.8 fusion.62
  2.3 0.7 convert_element_type.65
  3.0 0.1 fusion.56
  3.2 0.1 eq.53
  3.3 0.0 copy-start.2
  3.3 0.1 fusion.47
  3.4 0.1 fusion.50
  3.5 1.5 %convolution_convert_fusion = bf16[16,16,2048]{2,1,0:T(8,128)(2,1)S(1)} fusion(bf16[128,2048]{1,0:T(8,128)(2,1)} %param.6, f32[16,128]{1,0:T(8,128)S(1)} %fusion.56, pred[16,128]{1,0:T(8,128)(4,1)S(1)} %compare_bitcast_fusion), kind=kOutput, calls=%fused_computation.11 | convolution fusion | flops 134807552 | bytes 1583104 | tf_op jit(solution)/shard_map/dot_general | solution.py:35
  5.0 0.2 pad.8
  5.2 0.0 copy-done.2
  5.3 0.4 fusion.11
  5.7 0.2 pad_maximum_fusion
  5.9 26.5 %all_to_all.10 = bf16[16,16,4096]{2,1,0:T(8,128)(2,1)S(1)} all-to-all(bf16[16,16,4096]{2,1,0:T(8,128)(2,1)S(1)} %pad_maximum_fusion), channel_id=1, replica_groups=mesh['far'=8,'near'=4,'core'=2,'expert'=16] {'expert'}, dimensions={0} | all-to-all | bytes 4194304 | tf_op jit(solution)/shard_map/all_to_all | solution.py:44
  32.4 0.0 copy-start.1
  32.4 0.0 copy-done
  32.4 0.0 copy-start.3
  32.4 1.0 fusion.2
  33.4 0.4 copy-done.1
  33.7 1.3 %copy-done.3 = bf16[1,768,2048]{2,1,0:T(8,128)(2,1)S(1)} copy-done((bf16[1,768,2048]{2,1,0:T(8,128)(2,1)S(1)}, bf16[1,768,2048]{2,1,0:T(8,128)(2,1)}, u32[]{:S(2)}) %copy-start.3) | copy-done | bytes 3145752
  35.0 0.0 copy-start.4
  35.0 1.1 fusion.20
  36.2 0.0 copy-done.4
  36.2 0.1 convert_element_type.79
  36.3 0.8 fusion.61
  37.1 0.1 reshape.64
  37.2 1.1 pad.9.clone
  38.3 5.9 %fusion.15 = bf16[256,2048]{1,0:T(8,128)(2,1)} fusion(bf16[256,2048]{1,0:T(8,128)(2,1)} %bitcast.71, bf16[1,2048,768]{2,1,0:T(8,128)(2,1)S(1)} %copy-done, bf16[1,768,2048]{2,1,0:T(8,128)(2,1)} %param.11, f32[256]{0:T(256)S(1)} %reshape.64, bf16[256,4096]{1,0:T(8,128)(2,1)} %bitcast.67, f32[256,768]{1,0:T(8,128)} %copy-done.4), kind=kOutput, calls=%fused_computation.15 | convolution fusion | flops 1616576512 | bytes 10224640 | tf_op jit(solution)/shard_map/dot_general | solution.py:63
  44.2 4.3 %all-to-all-start.1 = ((bf16[16,16,2048]{2,1,0:T(8,128)(2,1)}), bf16[16,16,2048]{2,1,0:T(8,128)(2,1)}, u32[]{:S(2)}, u32[]{:S(2)}) async-start(bf16[16,16,2048]{2,1,0:T(8,128)(2,1)} %bitcast.70), calls=%async_computation.1 | async-start | bytes 2097152 | tf_op jit(solution)/shard_map/all_to_all | solution.py:70
  48.5 1.5 %multiply_reduce_fusion = f32[2048]{0:T(1024)S(1)} fusion(f32[256]{0:T(256)S(1)} %fusion.20, bf16[256,4096]{1,0:T(8,128)(2,1)} %bitcast.68), kind=kLoop, calls=%fused_computation.19 | loop fusion | flops 1570816 | bytes 1057792 | tf_op jit(solution)/shard_map/reduce_sum | solution.py:56
  50.0 44.0 %psum.21 = f32[2048]{0:T(1024)S(1)} all-reduce(f32[2048]{0:T(1024)S(1)} %multiply_reduce_fusion), channel_id=1, replica_groups=mesh['far'=8,'near'=4,'core'=2,'expert'=16] {'far'}, use_global_device_ids=true, to_apply=%region_5.6 | all-reduce | flops 2048 | bytes 16384 | tf_op jit(solution)/shard_map/psum | solution.py:10
  94.1 8.4 %psum.22 = f32[2048]{0:T(1024)S(1)} all-reduce(f32[2048]{0:T(1024)S(1)} %psum.21), channel_id=1, replica_groups=mesh['far'=8,'near'=4,'core'=2,'expert'=16] {'near'}, use_global_device_ids=true, to_apply=%region_6.7 | all-reduce | flops 2048 | bytes 16384 | tf_op jit(solution)/shard_map/psum | solution.py:10
  102.5 9.5 %psum.23 = f32[2048]{0:T(1024)S(1)} all-reduce(f32[2048]{0:T(1024)S(1)} %psum.22), channel_id=1, replica_groups=mesh['far'=8,'near'=4,'core'=2,'expert'=16] {'core'}, use_global_device_ids=true, to_apply=%region_7.8 | all-reduce | flops 2048 | bytes 16384 | tf_op jit(solution)/shard_map/psum | solution.py:10
  111.9 0.6 broadcast_multiply_fusion
  112.5 0.0 all-to-all-done.1
  112.5 0.9 fusion.44
  113.4 0.6 select_reduce_fusion
  114.1 2.4 %fusion.18 = bf16[128,2048]{1,0:T(8,128)(2,1)} fusion(bf16[16,16,2048]{2,1,0:T(8,128)(2,1)} %all-to-all-done.1, f32[16,128]{1,0:T(8,128)S(1)} %fusion.56, pred[16,128]{1,0:T(8,128)(4,1)S(1)} %compare_bitcast_fusion), kind=kOutput, calls=%fused_computation.16 | convolution fusion | flops 134545408 | bytes 1583104 | tf_op jit(solution)/shard_map/dot_general | solution.py:79
  (4 shorter events, 0.1 us)
Async XLA Ops:
  0.6 31.8 %copy-start = (bf16[1,2048,768]{2,1,0:T(8,128)(2,1)S(1)}, bf16[1,2048,768]{2,1,0:T(8,128)(2,1)}, u32[]{:S(2)}) copy-start(bf16[1,2048,768]{2,1,0:T(8,128)(2,1)} %param.10) | copy-start | bytes 9437188
  3.3 2.0 %copy-start.2 = (bf16[128,2048]{1,0:T(8,128)(2,1)S(1)}, bf16[128,2048]{1,0:T(8,128)(2,1)}, u32[]{:S(2)}) copy-start(bf16[128,2048]{1,0:T(8,128)(2,1)} %param.7) | copy-start | bytes 1572868
  32.4 1.4 %copy-start.1 = (bf16[16,16,4096]{2,1,0:T(8,128)(2,1)}, bf16[16,16,4096]{2,1,0:T(8,128)(2,1)S(1)}, u32[]{:S(2)}) copy-start(bf16[16,16,4096]{2,1,0:T(8,128)(2,1)S(1)} %all_to_all.10) | copy-start | bytes 6291460
  32.4 2.6 %copy-start.3 = (bf16[1,768,2048]{2,1,0:T(8,128)(2,1)S(1)}, bf16[1,768,2048]{2,1,0:T(8,128)(2,1)}, u32[]{:S(2)}) copy-start(bf16[1,768,2048]{2,1,0:T(8,128)(2,1)} %param.11) | copy-start | bytes 9437188
  35.0 1.1 copy-start.4
  44.2 68.4 %all-to-all-start.1 = ((bf16[16,16,2048]{2,1,0:T(8,128)(2,1)}), bf16[16,16,2048]{2,1,0:T(8,128)(2,1)}, u32[]{:S(2)}, u32[]{:S(2)}) async-start(bf16[16,16,2048]{2,1,0:T(8,128)(2,1)} %bitcast.70), calls=%async_computation.1 | async-start | bytes 2097152 | tf_op jit(solution)/shard_map/all_to_all | solution.py:70

commit v10 on v9

--- a/solution.py
+++ b/solution.py
@@ -7,7 +7,7 @@
 
 
 def dp_sum(local_col):
-    return lax.psum(lax.psum(lax.psum(local_col, "far"), "near"), "core")
+    return lax.psum(lax.psum(lax.psum(lax.psum(local_col, "core"), "pair"), "quad"), "far")
 
 
 def body(tokens, upstream, expert_ids, gate_weights, w_up, w_down):
@@ -15,7 +15,7 @@
     experts = EXP_DEV * owners
     tok_count, top = expert_ids.shape
     width = tokens.shape[1]
-    column_tok = tok_count * lax.axis_size(("far", "near", "core"))
+    column_tok = tok_count * lax.axis_size(("far", "quad", "pair", "core"))
     most = tok_count * top // experts + tok_count * top // (4 * experts)
     slots = -(-(most + 1) // 8) * 8
     rows_all = owners * slots
@@ -88,9 +88,9 @@
 
 def solution(mesh):
     n_dp = mesh.shape["dp"]
-    rows = ("far", "near", "core", "expert")
+    rows = ("far", "quad", "pair", "core", "expert")
     split = Mesh(
-        mesh.devices.reshape(n_dp // 8, 4, 2, mesh.shape["expert"]), rows
+        mesh.devices.reshape(n_dp // 8, 2, 2, 2, mesh.shape["expert"]), rows
     )
     return jax.shard_map(
         body,

time: 117 us -> 117 us (level)
  the two profiles are of different devices: /device:TPU:1 before, /device:TPU:2 now
where the time goes in v10:
time: 117 us; the launch traced here: 116 us
  blocking collectives  86.8 us (74%)
  matrix products  13.5 us (12%)
  other arithmetic  6.22 us (5%)
  starting transfers between devices  5.48 us (5%)
  local copies, waits for them, and re-layouts  3.27 us (3%)
    psum x1, blocking collectives, dp_sum(): lax.psum(lax.psum(lax.psum(lax.psum(local_col, 'core'), 'pair'), 'quad'),...  38.8 us
    all_to_all x1, blocking collectives, body(): lax.all_to_all(packed.reshape(owners, slots, -1), 'expert', 0, 0, tiled=T...  34.6 us
    psum x1, blocking collectives, dp_sum(): lax.psum(lax.psum(lax.psum(local_col, 'core'), 'pair'), 'quad')  6.02 us
    dot_general x1, matrix products, body(): lax.dot_general(act_grad, up_mat, (((1,), (1,)), ((), ())), preferred_ele...  5.9 us
    all_to_all x1, starting transfers between devices, body(): lax.all_to_all((route_grad + gate_back).reshape(owners, slots, -1), 'expe...  5.48 us
    psum x1, blocking collectives, dp_sum(): lax.psum(lax.psum(local_col, 'core'), 'pair')  4.98 us
    psum x1, blocking collectives, dp_sum(): lax.psum(local_col, 'core')  2.5 us
    dot_general x1, matrix products, body(): lax.dot_general(pick, back_rows, (((0,), (0,)), ((), ())), preferred_elem...  2.38 us
  transfers between devices with their start and end apart: 1, of which 0 were waited for; matrix products, arithmetic and copies ran while one was open for 2% of the time, Pallas kernels for 0%

profile of v10, /device:TPU:2, one launch (start us, length us, event | category | flops | bytes accessed | tf_op | source)
XLA Modules:
  0.0 116.0 jit_solution(15615911731077878245)
XLA Ops:
  0.6 0.0 copy-start
  0.6 0.8 add_select_fusion.1
  1.5 0.8 fusion.62
  2.3 0.7 convert_element_type.65
  3.0 0.1 fusion.56
  3.2 0.1 eq.53
  3.3 0.0 copy-start.2
  3.3 0.1 fusion.47
  3.4 0.1 fusion.50
  3.5 1.5 %convolution_convert_fusion = bf16[16,16,2048]{2,1,0:T(8,128)(2,1)S(1)} fusion(bf16[128,2048]{1,0:T(8,128)(2,1)} %param.6, f32[16,128]{1,0:T(8,128)S(1)} %fusion.56, pred[16,128]{1,0:T(8,128)(4,1)S(1)} %compare_bitcast_fusion), kind=kOutput, calls=%fused_computation.11 | convolution fusion | flops 134807552 | bytes 1583104 | tf_op jit(solution)/shard_map/dot_general | solution.py:35
  5.0 0.2 pad.8
  5.2 0.0 copy-done.2
  5.3 0.4 fusion.11
  5.7 0.2 pad_maximum_fusion
  5.9 34.6 %all_to_all.10 = bf16[16,16,4096]{2,1,0:T(8,128)(2,1)S(1)} all-to-all(bf16[16,16,4096]{2,1,0:T(8,128)(2,1)S(1)} %pad_maximum_fusion), channel_id=1, replica_groups=mesh['far'=8,'quad'=2,'pair'=2,'core'=2,'expert'=16] {'expert'}, dimensions={0} | all-to-all | bytes 4194304 | tf_op jit(solution)/shard_map/all_to_all | solution.py:44
  40.5 0.0 copy-start.1
  40.5 0.0 copy-done
  40.5 0.0 copy-start.3
  40.5 1.0 fusion.2
  41.5 0.4 copy-done.1
  41.8 1.3 %copy-done.3 = bf16[1,768,2048]{2,1,0:T(8,128)(2,1)S(1)} copy-done((bf16[1,768,2048]{2,1,0:T(8,128)(2,1)S(1)}, bf16[1,768,2048]{2,1,0:T(8,128)(2,1)}, u32[]{:S(2)}) %copy-start.3) | copy-done | bytes 3145752
  43.1 0.0 copy-start.4
  43.1 1.1 fusion.20
  44.2 0.0 copy-done.4
  44.3 0.1 convert_element_type.79
  44.4 0.8 fusion.61
  45.1 0.1 reshape.64
  45.2 1.1 pad.9.clone
  46.3 5.9 %fusion.15 = bf16[256,2048]{1,0:T(8,128)(2,1)} fusion(bf16[256,2048]{1,0:T(8,128)(2,1)} %bitcast.71, bf16[1,2048,768]{2,1,0:T(8,128)(2,1)S(1)} %copy-done, bf16[1,768,2048]{2,1,0:T(8,128)(2,1)} %param.11, f32[256]{0:T(256)S(1)} %reshape.64, bf16[256,4096]{1,0:T(8,128)(2,1)} %bitcast.67, f32[256,768]{1,0:T(8,128)} %copy-done.4), kind=kOutput, calls=%fused_computation.15 | convolution fusion | flops 1616576512 | bytes 10224640 | tf_op jit(solution)/shard_map/dot_general | solution.py:63
  52.2 5.5 %all-to-all-start.1 = ((bf16[16,16,2048]{2,1,0:T(8,128)(2,1)}), bf16[16,16,2048]{2,1,0:T(8,128)(2,1)}, u32[]{:S(2)}, u32[]{:S(2)}) async-start(bf16[16,16,2048]{2,1,0:T(8,128)(2,1)} %bitcast.70), calls=%async_computation.1 | async-start | bytes 2097152 | tf_op jit(solution)/shard_map/all_to_all | solution.py:70
  57.7 1.5 %multiply_reduce_fusion = f32[2048]{0:T(1024)S(1)} fusion(f32[256]{0:T(256)S(1)} %fusion.20, bf16[256,4096]{1,0:T(8,128)(2,1)} %bitcast.68), kind=kLoop, calls=%fused_computation.19 | loop fusion | flops 1570816 | bytes 1057792 | tf_op jit(solution)/shard_map/reduce_sum | solution.py:56
  59.2 2.5 %psum.28 = f32[2048]{0:T(1024)S(1)} all-reduce(f32[2048]{0:T(1024)S(1)} %multiply_reduce_fusion), channel_id=1, replica_groups=mesh['far'=8,'quad'=2,'pair'=2,'core'=2,'expert'=16] {'core'}, use_global_device_ids=true, to_apply=%region_5.6 | all-reduce | flops 2048 | bytes 16384 | tf_op jit(solution)/shard_map/psum | solution.py:10
  61.7 5.0 %psum.29 = f32[2048]{0:T(1024)S(1)} all-reduce(f32[2048]{0:T(1024)S(1)} %psum.28), channel_id=1, replica_groups=mesh['far'=8,'quad'=2,'pair'=2,'core'=2,'expert'=16] {'pair'}, use_global_device_ids=true, to_apply=%region_6.7 | all-reduce | flops 2048 | bytes 16384 | tf_op jit(solution)/shard_map/psum | solution.py:10
  66.7 6.0 %psum.30 = f32[2048]{0:T(1024)S(1)} all-reduce(f32[2048]{0:T(1024)S(1)} %psum.29), channel_id=1, replica_groups=mesh['far'=8,'quad'=2,'pair'=2,'core'=2,'expert'=16] {'quad'}, use_global_device_ids=true, to_apply=%region_7.8 | all-reduce | flops 2048 | bytes 16384 | tf_op jit(solution)/shard_map/psum | solution.py:10
  72.7 38.8 %psum.31 = f32[2048]{0:T(1024)S(1)} all-reduce(f32[2048]{0:T(1024)S(1)} %psum.30), channel_id=1, replica_groups=mesh['far'=8,'quad'=2,'pair'=2,'core'=2,'expert'=16] {'far'}, use_global_device_ids=true, to_apply=%region_8.9 | all-reduce | flops 2048 | bytes 16384 | tf_op jit(solution)/shard_map/psum | solution.py:10
  111.5 0.6 broadcast_multiply_fusion
  112.1 0.0 all-to-all-done.1
  112.1 0.9 fusion.44
  113.0 0.6 select_reduce_fusion
  113.6 2.4 %fusion.18 = bf16[128,2048]{1,0:T(8,128)(2,1)} fusion(bf16[16,16,2048]{2,1,0:T(8,128)(2,1)} %all-to-all-done.1, f32[16,128]{1,0:T(8,128)S(1)} %fusion.56, pred[16,128]{1,0:T(8,128)(4,1)S(1)} %compare_bitcast_fusion), kind=kOutput, calls=%fused_computation.16 | convolution fusion | flops 134545408 | bytes 1583104 | tf_op jit(solution)/shard_map/dot_general | solution.py:79
  (4 shorter events, 0.1 us)
Async XLA Ops:
  0.6 39.8 %copy-start = (bf16[1,2048,768]{2,1,0:T(8,128)(2,1)S(1)}, bf16[1,2048,768]{2,1,0:T(8,128)(2,1)}, u32[]{:S(2)}) copy-start(bf16[1,2048,768]{2,1,0:T(8,128)(2,1)} %param.10) | copy-start | bytes 9437188
  3.3 2.0 %copy-start.2 = (bf16[128,2048]{1,0:T(8,128)(2,1)S(1)}, bf16[128,2048]{1,0:T(8,128)(2,1)}, u32[]{:S(2)}) copy-start(bf16[128,2048]{1,0:T(8,128)(2,1)} %param.7) | copy-start | bytes 1572868
  40.5 1.4 %copy-start.1 = (bf16[16,16,4096]{2,1,0:T(8,128)(2,1)}, bf16[16,16,4096]{2,1,0:T(8,128)(2,1)S(1)}, u32[]{:S(2)}) copy-start(bf16[16,16,4096]{2,1,0:T(8,128)(2,1)S(1)} %all_to_all.10) | copy-start | bytes 6291460
  40.5 2.6 %copy-start.3 = (bf16[1,768,2048]{2,1,0:T(8,128)(2,1)S(1)}, bf16[1,768,2048]{2,1,0:T(8,128)(2,1)}, u32[]{:S(2)}) copy-start(bf16[1,768,2048]{2,1,0:T(8,128)(2,1)} %param.11) | copy-start | bytes 9437188
  43.1 1.1 copy-start.4
  52.2 59.9 %all-to-all-start.1 = ((bf16[16,16,2048]{2,1,0:T(8,128)(2,1)}), bf16[16,16,2048]{2,1,0:T(8,128)(2,1)}, u32[]{:S(2)}, u32[]{:S(2)}) async-start(bf16[16,16,2048]{2,1,0:T(8,128)(2,1)} %bitcast.70), calls=%async_computation.1 | async-start | bytes 2097152 | tf_op jit(solution)/shard_map/all_to_all | solution.py:70

commit v11 on v7

--- a/solution.py
+++ b/solution.py
@@ -21,9 +21,7 @@
     rows_all = owners * slots
     up_mat = w_up[0]
     down_mat = w_down[0]
-    live = expert_ids % EXP_DEV == 0
-    target = expert_ids // EXP_DEV
-    hit = (target[:, :, None] == jnp.arange(owners)[None, None, :]) & live[:, :, None]
+    hit = expert_ids[:, :, None] == (EXP_DEV * jnp.arange(owners))[None, None, :]
     hit_f = hit.astype(jnp.float32)
     tok_oh = jnp.sum(hit_f, axis=1)
     lower = (jnp.arange(tok_count)[None, :] < jnp.arange(tok_count)[:, None]).astype(jnp.float32)

time: 116 us -> 116 us (level)
  no operation moved by 1% of the time
where the time goes in v11:
time: 116 us; the launch traced here: 115 us
  blocking collectives  86.4 us (74%)
  matrix products  13.5 us (12%)
  other arithmetic  5.62 us (5%)
  starting transfers between devices  5.61 us (5%)
  local copies, waits for them, and re-layouts  3.27 us (3%)
    psum x3, blocking collectives, dp_sum(): return lax.psum(lax.psum(lax.psum(local_col, 'core'), 'near'), 'far')  51.8 us
    all_to_all x1, blocking collectives, body(): lax.all_to_all(packed.reshape(owners, slots, -1), 'expert', 0, 0, tiled=T...  34.6 us
    dot_general x1, matrix products, body(): lax.dot_general(act_grad, up_mat, (((1,), (1,)), ((), ())), preferred_ele...  5.9 us
    all_to_all x1, starting transfers between devices, body(): lax.all_to_all((route_grad + gate_back).reshape(owners, slots, -1), 'expe...  5.61 us
    dot_general x1, matrix products, body(): lax.dot_general(pick, back_rows, (((0,), (0,)), ((), ())), preferred_elem...  2.38 us
  transfers between devices with their start and end apart: 1, of which 0 were waited for; matrix products, arithmetic and copies ran while one was open for 2% of the time, Pallas kernels for 0%

profile of v11, /device:TPU:2, one launch (start us, length us, event | category | flops | bytes accessed | tf_op | source)
XLA Modules:
  0.0 115.1 jit_solution(2610262230172237880)
XLA Ops:
  0.6 0.0 copy-start
  0.7 0.8 convert_element_type.65
  1.5 0.9 fusion.51
  2.4 0.1 fusion.58
  2.5 0.1 eq.46
  2.6 0.0 copy-start.2
  2.6 0.1 fusion.47
  2.8 0.1 fusion.50
  2.9 1.5 %convolution_convert_fusion = bf16[16,16,2048]{2,1,0:T(8,128)(2,1)S(1)} fusion(bf16[128,2048]{1,0:T(8,128)(2,1)} %param.6, f32[16,128]{1,0:T(8,128)S(1)} %fusion.58, pred[16,128]{1,0:T(8,128)(4,1)S(1)} %compare_bitcast_fusion), kind=kOutput, calls=%fused_computation.11 | convolution fusion | flops 134807552 | bytes 1583104 | tf_op jit(solution)/shard_map/dot_general | solution.py:33
  4.4 0.2 pad.8
  4.6 0.0 copy-done.2
  4.6 0.4 fusion.11
  5.0 0.2 pad_maximum_fusion
  5.3 34.6 %all_to_all.10 = bf16[16,16,4096]{2,1,0:T(8,128)(2,1)S(1)} all-to-all(bf16[16,16,4096]{2,1,0:T(8,128)(2,1)S(1)} %pad_maximum_fusion), channel_id=1, replica_groups=mesh['far'=8,'near'=4,'core'=2,'expert'=16] {'expert'}, dimensions={0} | all-to-all | bytes 4194304 | tf_op jit(solution)/shard_map/all_to_all | solution.py:42
  39.8 0.0 copy-start.1
  39.8 0.0 copy-done
  39.8 0.0 copy-start.4
  39.8 1.0 fusion.2
  40.8 0.4 copy-done.1
  41.2 1.3 %copy-done.4 = bf16[1,768,2048]{2,1,0:T(8,128)(2,1)S(1)} copy-done((bf16[1,768,2048]{2,1,0:T(8,128)(2,1)S(1)}, bf16[1,768,2048]{2,1,0:T(8,128)(2,1)}, u32[]{:S(2)}) %copy-start.4) | copy-done | bytes 3145752
  42.5 0.0 copy-start.5
  42.5 1.1 fusion.20
  43.6 0.0 copy-done.5
  43.6 0.1 convert_element_type.79
  43.7 0.8 fusion.63
  44.5 0.1 reshape.67
  44.6 1.1 pad.9.clone
  45.7 5.9 %fusion.15 = bf16[256,2048]{1,0:T(8,128)(2,1)} fusion(bf16[256,2048]{1,0:T(8,128)(2,1)} %bitcast.71, bf16[1,2048,768]{2,1,0:T(8,128)(2,1)S(1)} %copy-done, bf16[1,768,2048]{2,1,0:T(8,128)(2,1)} %param.11, f32[256]{0:T(256)S(1)} %reshape.67, bf16[256,4096]{1,0:T(8,128)(2,1)} %bitcast.67, f32[256,768]{1,0:T(8,128)} %copy-done.5), kind=kOutput, calls=%fused_computation.15 | convolution fusion | flops 1616576512 | bytes 10224640 | tf_op jit(solution)/shard_map/dot_general | solution.py:61
  51.6 0.0 copy-start.3
  51.6 5.6 %all-to-all-start.1 = ((bf16[16,16,2048]{2,1,0:T(8,128)(2,1)}), bf16[16,16,2048]{2,1,0:T(8,128)(2,1)}, u32[]{:S(2)}, u32[]{:S(2)}) async-start(bf16[16,16,2048]{2,1,0:T(8,128)(2,1)} %bitcast.70), calls=%async_computation.1 | async-start | bytes 2097152 | tf_op jit(solution)/shard_map/all_to_all | solution.py:68
  57.2 1.5 %multiply_reduce_fusion = f32[2048]{0:T(1024)S(1)} fusion(f32[256]{0:T(256)S(1)} %fusion.20, bf16[256,4096]{1,0:T(8,128)(2,1)} %bitcast.68), kind=kLoop, calls=%fused_computation.19 | loop fusion | flops 1570816 | bytes 1057792 | tf_op jit(solution)/shard_map/reduce_sum | solution.py:54
  58.7 2.5 %psum.21 = f32[2048]{0:T(1024)S(1)} all-reduce(f32[2048]{0:T(1024)S(1)} %multiply_reduce_fusion), channel_id=1, replica_groups=mesh['far'=8,'near'=4,'core'=2,'expert'=16] {'core'}, use_global_device_ids=true, to_apply=%region_5.6 | all-reduce | flops 2048 | bytes 16384 | tf_op jit(solution)/shard_map/psum | solution.py:10
  61.2 12.9 %psum.22 = f32[2048]{0:T(1024)S(1)} all-reduce(f32[2048]{0:T(1024)S(1)} %psum.21), channel_id=1, replica_groups=mesh['far'=8,'near'=4,'core'=2,'expert'=16] {'near'}, use_global_device_ids=true, to_apply=%region_6.7 | all-reduce | flops 2048 | bytes 16384 | tf_op jit(solution)/shard_map/psum | solution.py:10
  74.2 36.4 %psum.23 = f32[2048]{0:T(1024)S(1)} all-reduce(f32[2048]{0:T(1024)S(1)} %psum.22), channel_id=1, replica_groups=mesh['far'=8,'near'=4,'core'=2,'expert'=16] {'far'}, use_global_device_ids=true, to_apply=%region_7.8 | all-reduce | flops 2048 | bytes 16384 | tf_op jit(solution)/shard_map/psum | solution.py:10
  110.6 0.6 broadcast_multiply_fusion
  111.2 0.0 all-to-all-done.1
  111.2 0.9 fusion.44
  112.1 0.0 copy-done.3
  112.1 0.7 fusion.53
  112.8 2.4 %fusion.18 = bf16[128,2048]{1,0:T(8,128)(2,1)} fusion(bf16[16,16,2048]{2,1,0:T(8,128)(2,1)} %all-to-all-done.1, f32[16,128]{1,0:T(8,128)S(1)} %fusion.58, pred[16,128]{1,0:T(8,128)(4,1)S(1)} %compare_bitcast_fusion), kind=kOutput, calls=%fused_computation.16 | convolution fusion | flops 134545408 | bytes 1583104 | tf_op jit(solution)/shard_map/dot_general | solution.py:77
  (4 shorter events, 0.0 us)
Async XLA Ops:
  0.6 39.2 %copy-start = (bf16[1,2048,768]{2,1,0:T(8,128)(2,1)S(1)}, bf16[1,2048,768]{2,1,0:T(8,128)(2,1)}, u32[]{:S(2)}) copy-start(bf16[1,2048,768]{2,1,0:T(8,128)(2,1)} %param.10) | copy-start | bytes 9437188
  2.6 2.0 %copy-start.2 = (bf16[128,2048]{1,0:T(8,128)(2,1)S(1)}, bf16[128,2048]{1,0:T(8,128)(2,1)}, u32[]{:S(2)}) copy-start(bf16[128,2048]{1,0:T(8,128)(2,1)} %param.7) | copy-start | bytes 1572868
  39.8 1.4 %copy-start.1 = (bf16[16,16,4096]{2,1,0:T(8,128)(2,1)}, bf16[16,16,4096]{2,1,0:T(8,128)(2,1)S(1)}, u32[]{:S(2)}) copy-start(bf16[16,16,4096]{2,1,0:T(8,128)(2,1)S(1)} %all_to_all.10) | copy-start | bytes 6291460
  39.8 2.6 %copy-start.4 = (bf16[1,768,2048]{2,1,0:T(8,128)(2,1)S(1)}, bf16[1,768,2048]{2,1,0:T(8,128)(2,1)}, u32[]{:S(2)}) copy-start(bf16[1,768,2048]{2,1,0:T(8,128)(2,1)} %param.11) | copy-start | bytes 9437188
  42.5 1.1 copy-start.5
  51.6 60.5 %copy-start.3 = (s32[128,8]{0,1:T(8,128)S(1)}, s32[128,8]{0,1:T(8,128)}, u32[]{:S(2)}) copy-start(s32[128,8]{0,1:T(8,128)} %param.8) | copy-start | bytes 12292
  51.6 59.6 %all-to-all-start.1 = ((bf16[16,16,2048]{2,1,0:T(8,128)(2,1)}), bf16[16,16,2048]{2,1,0:T(8,128)(2,1)}, u32[]{:S(2)}, u32[]{:S(2)}) async-start(bf16[16,16,2048]{2,1,0:T(8,128)(2,1)} %bitcast.70), calls=%async_computation.1 | async-start | bytes 2097152 | tf_op jit(solution)/shard_map/all_to_all | solution.py:68

commit v12 on v11

--- a/solution.py
+++ b/solution.py
@@ -29,7 +29,9 @@
     slot_hit = before.T[:, None, :] == jnp.arange(slots, dtype=jnp.float32)[None, :, None]
     pick3 = slot_hit & (tok_oh.T[:, None, :] > 0)
     pick = pick3.reshape(rows_all, tok_count).astype(jnp.bfloat16)
-    gate_tc = jnp.sum(hit_f * gate_weights.astype(jnp.float32)[:, :, None], axis=1)
+    gate_tc = jnp.sum(
+        jnp.where(hit, gate_weights[:, :, None], jnp.zeros((), gate_weights.dtype)), axis=1
+    ).astype(jnp.float32)
     send_x = jnp.dot(pick, tokens, preferred_element_type=jnp.float32)
     send_dy = jnp.dot(pick, upstream, preferred_element_type=jnp.float32)
     send_gate = jnp.einsum(

time: 116 us -> 116 us (level)
  no operation moved by 1% of the time
where the time goes in v12:
time: 116 us; the launch traced here: 115 us
  blocking collectives  86.4 us (74%)
  matrix products  13.5 us (12%)
  other arithmetic  5.63 us (5%)
  starting transfers between devices  5.61 us (5%)
  local copies, waits for them, and re-layouts  3.26 us (3%)
    psum x3, blocking collectives, dp_sum(): return lax.psum(lax.psum(lax.psum(local_col, 'core'), 'near'), 'far')  51.8 us
    all_to_all x1, blocking collectives, body(): lax.all_to_all(packed.reshape(owners, slots, -1), 'expert', 0, 0, tiled=T...  34.6 us
    dot_general x1, matrix products, body(): lax.dot_general(act_grad, up_mat, (((1,), (1,)), ((), ())), preferred_ele...  5.9 us
    all_to_all x1, starting transfers between devices, body(): lax.all_to_all((route_grad + gate_back).reshape(owners, slots, -1), 'expe...  5.61 us
    dot_general x1, matrix products, body(): lax.dot_general(pick, back_rows, (((0,), (0,)), ((), ())), preferred_elem...  2.38 us
  transfers between devices with their start and end apart: 1, of which 0 were waited for; matrix products, arithmetic and copies ran while one was open for 2% of the time, Pallas kernels for 0%

profile of v12, /device:TPU:2, one launch (start us, length us, event | category | flops | bytes accessed | tf_op | source)
XLA Modules:
  0.0 115.1 jit_solution(18305029730971907473)
XLA Ops:
  0.6 0.0 copy-start
  0.7 0.9 fusion.51
  1.6 0.1 fusion.57
  1.7 0.8 fusion.62
  2.5 0.1 eq.46
  2.6 0.0 copy-start.2
  2.6 0.1 fusion.47
  2.8 0.1 fusion.50
  2.9 1.5 %convolution_convert_fusion = bf16[16,16,2048]{2,1,0:T(8,128)(2,1)S(1)} fusion(bf16[128,2048]{1,0:T(8,128)(2,1)} %param.6, f32[16,128]{1,0:T(8,128)S(1)} %fusion.57, pred[16,128]{1,0:T(8,128)(4,1)S(1)} %compare_bitcast_fusion), kind=kOutput, calls=%fused_computation.11 | convolution fusion | flops 134807552 | bytes 1583104 | tf_op jit(solution)/shard_map/dot_general | solution.py:35
  4.4 0.2 pad.8
  4.6 0.0 copy-done.2
  4.6 0.4 fusion.11
  5.0 0.2 pad_maximum_fusion
  5.2 34.6 %all_to_all.10 = bf16[16,16,4096]{2,1,0:T(8,128)(2,1)S(1)} all-to-all(bf16[16,16,4096]{2,1,0:T(8,128)(2,1)S(1)} %pad_maximum_fusion), channel_id=1, replica_groups=mesh['far'=8,'near'=4,'core'=2,'expert'=16] {'expert'}, dimensions={0} | all-to-all | bytes 4194304 | tf_op jit(solution)/shard_map/all_to_all | solution.py:44
  39.8 0.0 copy-start.1
  39.8 0.0 copy-done
  39.8 0.0 copy-start.4
  39.8 1.0 fusion.2
  40.8 0.4 copy-done.1
  41.2 1.3 %copy-done.4 = bf16[1,768,2048]{2,1,0:T(8,128)(2,1)S(1)} copy-done((bf16[1,768,2048]{2,1,0:T(8,128)(2,1)S(1)}, bf16[1,768,2048]{2,1,0:T(8,128)(2,1)}, u32[]{:S(2)}) %copy-start.4) | copy-done | bytes 3145752
  42.5 0.0 copy-start.5
  42.5 1.1 fusion.20
  43.6 0.0 copy-done.5
  43.6 0.1 convert_element_type.78
  43.7 0.8 fusion.63
  44.5 0.1 reshape.67
  44.6 1.1 pad.9.clone
  45.7 5.9 %fusion.15 = bf16[256,2048]{1,0:T(8,128)(2,1)} fusion(bf16[256,2048]{1,0:T(8,128)(2,1)} %bitcast.68, bf16[1,2048,768]{2,1,0:T(8,128)(2,1)S(1)} %copy-done, bf16[1,768,2048]{2,1,0:T(8,128)(2,1)} %param.11, f32[256]{0:T(256)S(1)} %reshape.67, bf16[256,4096]{1,0:T(8,128)(2,1)} %bitcast.64, f32[256,768]{1,0:T(8,128)} %copy-done.5), kind=kOutput, calls=%fused_computation.15 | convolution fusion | flops 1616576512 | bytes 10224640 | tf_op jit(solution)/shard_map/dot_general | solution.py:63
  51.6 0.0 copy-start.3
  51.6 5.6 %all-to-all-start.1 = ((bf16[16,16,2048]{2,1,0:T(8,128)(2,1)}), bf16[16,16,2048]{2,1,0:T(8,128)(2,1)}, u32[]{:S(2)}, u32[]{:S(2)}) async-start(bf16[16,16,2048]{2,1,0:T(8,128)(2,1)} %bitcast.67), calls=%async_computation.1 | async-start | bytes 2097152 | tf_op jit(solution)/shard_map/all_to_all | solution.py:70
  57.2 1.5 %multiply_reduce_fusion = f32[2048]{0:T(1024)S(1)} fusion(f32[256]{0:T(256)S(1)} %fusion.20, bf16[256,4096]{1,0:T(8,128)(2,1)} %bitcast.65), kind=kLoop, calls=%fused_computation.19 | loop fusion | flops 1570816 | bytes 1057792 | tf_op jit(solution)/shard_map/reduce_sum | solution.py:56
  58.7 2.5 %psum.21 = f32[2048]{0:T(1024)S(1)} all-reduce(f32[2048]{0:T(1024)S(1)} %multiply_reduce_fusion), channel_id=1, replica_groups=mesh['far'=8,'near'=4,'core'=2,'expert'=16] {'core'}, use_global_device_ids=true, to_apply=%region_5.6 | all-reduce | flops 2048 | bytes 16384 | tf_op jit(solution)/shard_map/psum | solution.py:10
  61.2 12.9 %psum.22 = f32[2048]{0:T(1024)S(1)} all-reduce(f32[2048]{0:T(1024)S(1)} %psum.21), channel_id=1, replica_groups=mesh['far'=8,'near'=4,'core'=2,'expert'=16] {'near'}, use_global_device_ids=true, to_apply=%region_6.7 | all-reduce | flops 2048 | bytes 16384 | tf_op jit(solution)/shard_map/psum | solution.py:10
  74.2 36.4 %psum.23 = f32[2048]{0:T(1024)S(1)} all-reduce(f32[2048]{0:T(1024)S(1)} %psum.22), channel_id=1, replica_groups=mesh['far'=8,'near'=4,'core'=2,'expert'=16] {'far'}, use_global_device_ids=true, to_apply=%region_7.8 | all-reduce | flops 2048 | bytes 16384 | tf_op jit(solution)/shard_map/psum | solution.py:10
  110.6 0.6 broadcast_multiply_fusion
  111.2 0.0 all-to-all-done.1
  111.2 0.9 fusion.44
  112.1 0.0 copy-done.3
  112.1 0.7 fusion.52
  112.7 2.4 %fusion.18 = bf16[128,2048]{1,0:T(8,128)(2,1)} fusion(bf16[16,16,2048]{2,1,0:T(8,128)(2,1)} %all-to-all-done.1, f32[16,128]{1,0:T(8,128)S(1)} %fusion.57, pred[16,128]{1,0:T(8,128)(4,1)S(1)} %compare_bitcast_fusion), kind=kOutput, calls=%fused_computation.16 | convolution fusion | flops 134545408 | bytes 1583104 | tf_op jit(solution)/shard_map/dot_general | solution.py:79
  (4 shorter events, 0.0 us)
Async XLA Ops:
  0.6 39.2 %copy-start = (bf16[1,2048,768]{2,1,0:T(8,128)(2,1)S(1)}, bf16[1,2048,768]{2,1,0:T(8,128)(2,1)}, u32[]{:S(2)}) copy-start(bf16[1,2048,768]{2,1,0:T(8,128)(2,1)} %param.10) | copy-start | bytes 9437188
  2.6 2.0 %copy-start.2 = (bf16[128,2048]{1,0:T(8,128)(2,1)S(1)}, bf16[128,2048]{1,0:T(8,128)(2,1)}, u32[]{:S(2)}) copy-start(bf16[128,2048]{1,0:T(8,128)(2,1)} %param.7) | copy-start | bytes 1572868
  39.8 1.4 %copy-start.1 = (bf16[16,16,4096]{2,1,0:T(8,128)(2,1)}, bf16[16,16,4096]{2,1,0:T(8,128)(2,1)S(1)}, u32[]{:S(2)}) copy-start(bf16[16,16,4096]{2,1,0:T(8,128)(2,1)S(1)} %all_to_all.10) | copy-start | bytes 6291460
  39.8 2.6 %copy-start.4 = (bf16[1,768,2048]{2,1,0:T(8,128)(2,1)S(1)}, bf16[1,768,2048]{2,1,0:T(8,128)(2,1)}, u32[]{:S(2)}) copy-start(bf16[1,768,2048]{2,1,0:T(8,128)(2,1)} %param.11) | copy-start | bytes 9437188
  42.5 1.1 copy-start.5
  51.6 60.5 %copy-start.3 = (s32[128,8]{0,1:T(8,128)S(1)}, s32[128,8]{0,1:T(8,128)}, u32[]{:S(2)}) copy-start(s32[128,8]{0,1:T(8,128)} %param.8) | copy-start | bytes 12292
  51.6 59.6 %all-to-all-start.1 = ((bf16[16,16,2048]{2,1,0:T(8,128)(2,1)}), bf16[16,16,2048]{2,1,0:T(8,128)(2,1)}, u32[]{:S(2)}, u32[]{:S(2)}) async-start(bf16[16,16,2048]{2,1,0:T(8,128)(2,1)} %bitcast.67), calls=%async_computation.1 | async-start | bytes 2097152 | tf_op jit(solution)/shard_map/all_to_all | solution.py:70
